TPU v7x, 512 devices: a whole 4x8x8 slice. The times are simulated.
512 devices in a mesh: req: 64 (over y, x, core), tp: 8 (over z).
Axes of the slice: x: 4, y: 8, z: 8, core: 2. Of those that a mesh axis runs over, the one named last changes fastest.
Arguments:
- tokens: bfloat16 [8192, 8192], P('req', 'tp'), may hold values from -6 to 6
- kv_weight: bfloat16 [8192, 1024], P('tp'), may hold values from -0.0625 to 0.0625
- queries: bfloat16 [8192, 4096], P('req', 'tp'), may hold values from -96 to 96, as said below
- lengths: int32 [32], replicated, may hold values from 1 to 384, 8192 in all
- page_owner: int32 [4096, 1], P('req'), may hold values from 0 to 63; in each aligned block of 64 rows (0 to 63, 64 to 127, ...) at most 2 rows name the same one
Outputs:
- attended: bfloat16 [8192, 4096], P('req', 'tp')
- cache: bfloat16 [16384, 1024], P('req', 'tp')
Inputs may be any that keep to these rules, and one draw needn't show every extreme that they name: `queries`: real values; entries of a row share a scale. The 32 lengths sum to 8192; the largest is exactly 384. `page_owner`: among the 64 pages of one device no owner is named more than 2 times, a bound that some block reaches.
All inputs are finite; a program needn't handle non-finite values.
Results may differ from a plain program's by a relative error of at most 0.012.
Values may be sent and summed in bfloat16 or wider, within the bound.
No kernel may reach another device: no remote copies, remote signals or barrier semaphores. Data moves between devices by JAX's collectives and lax.ppermute only.
A program may use at most 64 MiB of HBM per device.

v0:
```python
import math

import jax
import jax.numpy as jnp
from jax import lax
from jax.sharding import PartitionSpec as P

HD = 128
HQ = 32
KVH = 4
BACK = 3


rope_base = 500000.0


def shifted(value, axis, steps):
    count = lax.axis_size(axis)
    first, last = (max(0, -steps), min(count, count - steps))
    return lax.ppermute(value, axis, [(source, source + steps) for source in range(first, last)])


def rotate(values, positions):
    middle = HD // 2
    frequency = rope_base ** (-(2.0 * jnp.arange(middle, dtype=jnp.float32)) / HD)
    angles = positions.astype(jnp.float32)[:, None] * frequency[None, :]
    cosine = jnp.cos(angles)[:, None, :]
    sine = jnp.sin(angles)[:, None, :]
    front = values[..., :middle]
    behind = values[..., middle:]
    return jnp.concatenate(
        [front * cosine - behind * sine, behind * cosine + front * sine], axis=-1
    )


def rotate_keys(block, positions):
    rows = block.shape[0]
    parts = block.shape[1] // HD
    shaped = block.reshape(rows, parts, HD)
    turned = rotate(shaped, positions)
    is_key = jnp.arange(parts, dtype=jnp.int32) % 2 == 0
    return jnp.where(is_key[None, :, None], turned, shaped).reshape(rows, parts * HD)


def segment_info(lengths, indices):
    ends = jnp.cumsum(lengths)
    before = ends[None, :] <= indices[:, None]
    segment = jnp.sum(before.astype(jnp.int32), axis=1)
    start = jnp.sum(jnp.where(before, lengths[None, :], 0), axis=1)
    return (segment, indices - start)


def local(tokens, kv_weight, queries, lengths, page_owner):
    rows = tokens.shape[0]
    columns = kv_weight.shape[1]
    share = columns // lax.axis_size("tp")
    tp_index = lax.axis_index("tp")
    req_index = lax.axis_index("req")
    local_index = req_index * rows + jnp.arange(rows, dtype=jnp.int32)
    segment, positions = segment_info(lengths, local_index)
    local_heads = queries.shape[1] // HD
    group = HQ // KVH
    per_group = min(local_heads, group)
    kv_count = local_heads // per_group
    first_head = tp_index * local_heads // group
    partial_value = jnp.dot(tokens, kv_weight, preferred_element_type=jnp.float32)
    summed = lax.psum(partial_value, "tp")
    cache_rows = rotate_keys(summed, positions).astype(jnp.bfloat16)
    mine = lax.dynamic_slice_in_dim(cache_rows, tp_index * share, share, 1)
    near = lax.dynamic_slice_in_dim(cache_rows, first_head * 2 * HD, kv_count * 2 * HD, 1)
    rotated = rotate(queries.astype(jnp.float32).reshape(rows, local_heads, HD), positions).astype(
        jnp.bfloat16
    )
    blocks = []
    for distance in range(BACK, 0, -1):
        blocks.append(shifted(near, "req", distance))
    blocks.append(near)
    window = jnp.concatenate(blocks, axis=0)
    key_total = (BACK + 1) * rows
    key_index = (req_index - BACK) * rows + jnp.arange(key_total, dtype=jnp.int32)
    key_segment, unused = segment_info(lengths, key_index)
    allowed = (
        (key_index[None, :] >= 0)
        & (key_index[None, :] <= local_index[:, None])
        & (key_segment[None, :] == segment[:, None])
    )
    key_parts = window.reshape(key_total, kv_count, 2, HD)
    head_keys = jnp.transpose(key_parts[:, :, 0, :], (1, 0, 2))
    head_values = jnp.transpose(key_parts[:, :, 1, :], (1, 0, 2))
    query_heads = jnp.transpose(rotated, (1, 0, 2))

    def attend_head(head):
        query_head = query_heads[head]
        slot = head // per_group
        key_head = head_keys[slot]
        value_head = head_values[slot]
        scores = lax.dot_general(
            query_head, key_head, (((1,), (1,)), ((), ())), preferred_element_type=jnp.float32
        ) / math.sqrt(HD)
        scores = jnp.where(allowed, scores, -1e30)
        largest = jnp.max(scores, axis=1, keepdims=True)
        weights = jnp.exp(scores - largest)
        total = jnp.sum(weights, axis=1, keepdims=True)
        mixed = jnp.dot(
            weights.astype(jnp.bfloat16), value_head, preferred_element_type=jnp.float32
        )
        return (mixed / total).astype(jnp.bfloat16)

    outputs = lax.map(attend_head, jnp.arange(local_heads, dtype=jnp.int32))
    attended = jnp.transpose(outputs, (1, 0, 2)).reshape(rows, local_heads * HD)
    pages_here = page_owner.shape[0]
    owners = page_owner[:, 0]
    page_rows = rows // pages_here
    capacity = 2 * pages_here // lax.axis_size("req")
    order = jnp.arange(pages_here, dtype=jnp.int32)
    earlier = (owners[:, None] == owners[None, :]) & (order[None, :] < order[:, None])
    rank = jnp.sum(earlier.astype(jnp.int32), axis=1)
    target = owners * capacity + rank
    slots = lax.axis_size("req") * capacity
    placing = (jnp.arange(slots, dtype=jnp.int32)[:, None] == target[None, :]).astype(jnp.bfloat16)
    paged = mine.reshape(pages_here, page_rows * share)
    outgoing = jnp.dot(placing, paged, preferred_element_type=jnp.float32).astype(jnp.bfloat16)
    incoming = lax.all_to_all(outgoing, "req", split_axis=0, concat_axis=0, tiled=True)
    cache = incoming.reshape(slots * page_rows, share)
    return (attended, cache)


def solution(mesh):
    in_specs = (P("req", "tp"), P("tp", None), P("req", "tp"), P(), P("req", None))
    out_specs = (P("req", "tp"), P("req", "tp"))
    return jax.shard_map(local, mesh=mesh, in_specs=in_specs, out_specs=out_specs, check_vma=False)
```

profile of v0, /device:TPU:1, one launch (start us, length us, event | category | flops | bytes accessed | tf_op | source)
XLA Modules:
  0.0 141.3 jit_solution(10183100208050448432)
XLA Ops:
  7.2 0.0 copy-start
  7.2 0.0 all-reduce.2.cloned.1.call-start
  7.3 1.5 %copy-done = bf16[1024,1024]{1,0:T(8,128)(2,1)S(1)} copy-done((bf16[1024,1024]{1,0:T(8,128)(2,1)S(1)}, bf16[1024,1024]{1,0:T(8,128)(2,1)}, u32[]{:S(2)}) %copy-start) | copy-done | bytes 2097176
  8.8 2.2 %fusion.23 = f32[128,1024]{1,0:T(8,128)} fusion(bf16[128,1024]{1,0:T(8,128)(2,1)} %param.7, bf16[1024,1024]{1,0:T(8,128)(2,1)S(1)} %copy-done), kind=kOutput, calls=%fused_computation.54 | convolution fusion | flops 268435456 | bytes 2883584 | tf_op jit(solution)/shard_map/dot_general | solution.py:66
  11.0 0.0 all-reduce.2.cloned.1.call-update
  11.1 0.1 copy.20
  11.2 0.1 reduce-window.8
  11.2 0.1 reduce
  11.3 0.1 fusion.19
  11.5 0.2 multiply_cosine_fusion
  11.7 0.1 copy.21
  11.8 0.1 copy.22
  11.9 0.1 copy.19
  12.1 0.1 convert_reduce_fusion
  12.2 0.2 convert_reduce_fusion.1
  12.4 0.1 broadcast_bitcast_fusion
  12.5 79.8 %all-reduce.2.cloned.1.call-done = f32[128,1024]{1,0:T(8,128)} async-done(((f32[128,1024]{1,0:T(8,128)}), f32[128,1024]{1,0:T(8,128)}) %all-reduce.2.cloned.1.call-update) | async-done | bytes 524304 | tf_op jit(solution)/shard_map/psum | solution.py:67
  92.2 1.2 copy.31
  93.5 0.3 multiply_subtract_fusion
  93.7 0.1 pad_maximum_fusion
  93.9 0.1 fusion.15
  94.0 9.6 %collective-permute-start = (bf16[128,256]{1,0:T(8,128)(2,1)S(1)}, bf16[128,256]{1,0:T(8,128)(2,1)S(1)}, u32[]{:S(2)}, u32[]{:S(2)}) collective-permute-start(bf16[128,256]{1,0:T(8,128)(2,1)S(1)} %constant_dynamic-slice_fusion.1), channel_id=1, source_target_pairs={{0,24},{8,32},{16,40},{24,48},{32,56},{40,64},{48,72},{56,80},{64,... | collective-permute-start | bytes 196616 | tf_op jit(solution)/shard_map/ppermute | solution.py:20
  103.6 2.2 %collective-permute-start.1 = (bf16[128,256]{1,0:T(8,128)(2,1)S(1)}, bf16[128,256]{1,0:T(8,128)(2,1)S(1)}, u32[]{:S(2)}, u32[]{:S(2)}) collective-permute-start(bf16[128,256]{1,0:T(8,128)(2,1)S(1)} %constant_dynamic-slice_fusion.1), channel_id=1, source_target_pairs={{0,16},{8,24},{16,32},{24,40},{32,48},{40,56},{48,64},{56,72},{64,... | collective-permute-start | bytes 196616 | tf_op jit(solution)/shard_map/ppermute | solution.py:20
  105.8 1.9 %collective-permute-start.2 = (bf16[128,256]{1,0:T(8,128)(2,1)S(1)}, bf16[128,256]{1,0:T(8,128)(2,1)S(1)}, u32[]{:S(2)}, u32[]{:S(2)}) collective-permute-start(bf16[128,256]{1,0:T(8,128)(2,1)S(1)} %constant_dynamic-slice_fusion.1), channel_id=1, source_target_pairs={{0,8},{8,16},{16,24},{24,32},{32,40},{40,48},{48,56},{56,64},{64,7... | collective-permute-start | bytes 196616 | tf_op jit(solution)/shard_map/ppermute | solution.py:20
  107.7 0.1 convolution_convert_fusion
  107.9 0.7 all_to_all.6
  108.6 9.9 %all-to-all-start = ((bf16[64,2,256]{2,1,0:T(2,128)(2,1)}), bf16[64,2,256]{2,1,0:T(2,128)(2,1)S(1)}, u32[]{:S(2)}, u32[]{:S(2)}) async-start(bf16[64,2,256]{2,1,0:T(2,128)(2,1)} %all_to_all.6), calls=%async_computation | async-start | bytes 131072 | tf_op jit(solution)/shard_map/all_to_all | solution.py:123
  118.5 0.1 reshape.160
  118.6 0.4 fusion.22
  119.0 14.1 %while.11 = (s32[]{:T(128)}, bf16[4,128,128]{2,1,0:T(8,128)(2,1)S(1)}, s32[4]{0:T(128)S(1)}, bf16[4,128,128]{1,2,0:T(8,128)(2,1)S(1)}, bf16[1,512,128]{2,1,0:T(8...) while((s32[]{:T(128)}, ...), condition=%wide.region_8.9_spmd.clone, body=%wide.region_5.8_spmd.clone.sunk | while | flops 34307844 | bytes 1122491 | solution.py:109
  119.1 0.7 dynamic_slice.30
  121.8 0.3 fusion.35
  122.1 0.2 fusion.36
  122.3 0.3 fusion.37
  122.6 0.7 dynamic_slice.30
  125.3 0.3 fusion.35
  125.6 0.2 fusion.36
  125.8 0.3 fusion.37
  126.1 0.7 dynamic_slice.30
  128.8 0.3 fusion.35
  129.1 0.2 fusion.36
  129.3 0.3 fusion.37
  129.6 0.7 dynamic_slice.30
  132.4 0.3 fusion.35
  132.7 0.2 fusion.36
  132.9 0.3 fusion.37
  133.1 0.7 copy_bitcast_fusion
  133.8 0.7 reshape.163
  (29 shorter events, 0.3 us)
Async XLA Ops:
  7.2 1.6 %copy-start = (bf16[1024,1024]{1,0:T(8,128)(2,1)S(1)}, bf16[1024,1024]{1,0:T(8,128)(2,1)}, u32[]{:S(2)}) copy-start(bf16[1024,1024]{1,0:T(8,128)(2,1)} %param.8) | copy-start | bytes 6291460
  7.2 3.9 %copy-start.3 = (s32[32]{0:T(128)S(1)}, s32[32]{0:T(128)}, u32[]{:S(2)}) copy-start(s32[32]{0:T(128)} %param.10) | copy-start | bytes 388
  7.2 4.7 %copy-start.2 = (bf16[128,512]{1,0:T(8,128)(2,1)S(1)}, bf16[128,512]{1,0:T(8,128)(2,1)}, u32[]{:S(2)}) copy-start(bf16[128,512]{1,0:T(8,128)(2,1)} %param.9) | copy-start | bytes 393220
  7.2 5.0 %copy-start.4 = (s32[64,1]{0,1:T(1,128)S(1)}, s32[64,1]{0,1:T(1,128)}, u32[]{:S(2)}) copy-start(s32[64,1]{0,1:T(1,128)} %param.11) | copy-start | bytes 772
  7.2 85.0 %all-reduce.2.cloned.1.call-start = ((), (), s32[]{:S(2)}) async-start(), calls=%async_computation.1 | async-start | bytes 1048576 | tf_op jit(solution)/shard_map/psum | solution.py:67
  92.2 1.6 %copy-start.1 = (f32[128,1024]{1,0:T(8,128)S(1)}, f32[128,1024]{1,0:T(8,128)}, u32[]{:S(2)}) copy-start(f32[128,1024]{1,0:T(8,128)} %all-reduce.2.cloned.1.call-done) | copy-start | bytes 1572868
  94.0 24.5 %collective-permute-start = (bf16[128,256]{1,0:T(8,128)(2,1)S(1)}, bf16[128,256]{1,0:T(8,128)(2,1)S(1)}, u32[]{:S(2)}, u32[]{:S(2)}) collective-permute-start(bf16[128,256]{1,0:T(8,128)(2,1)S(1)} %constant_dynamic-slice_fusion.1), channel_id=1, source_target_pairs={{0,24},{8,32},{16,40},{24,48},{32,56},{40,64},{48,72},{56,80},{64,... | collective-permute-start | bytes 196616 | tf_op jit(solution)/shard_map/ppermute | solution.py:20
  103.6 14.9 %collective-permute-start.1 = (bf16[128,256]{1,0:T(8,128)(2,1)S(1)}, bf16[128,256]{1,0:T(8,128)(2,1)S(1)}, u32[]{:S(2)}, u32[]{:S(2)}) collective-permute-start(bf16[128,256]{1,0:T(8,128)(2,1)S(1)} %constant_dynamic-slice_fusion.1), channel_id=1, source_target_pairs={{0,16},{8,24},{16,32},{24,40},{32,48},{40,56},{48,64},{56,72},{64,... | collective-permute-start | bytes 196616 | tf_op jit(solution)/shard_map/ppermute | solution.py:20
  105.8 12.7 %collective-permute-start.2 = (bf16[128,256]{1,0:T(8,128)(2,1)S(1)}, bf16[128,256]{1,0:T(8,128)(2,1)S(1)}, u32[]{:S(2)}, u32[]{:S(2)}) collective-permute-start(bf16[128,256]{1,0:T(8,128)(2,1)S(1)} %constant_dynamic-slice_fusion.1), channel_id=1, source_target_pairs={{0,8},{8,16},{16,24},{24,32},{32,40},{40,48},{48,56},{56,64},{64,7... | collective-permute-start | bytes 196616 | tf_op jit(solution)/shard_map/ppermute | solution.py:20
  108.6 25.2 %all-to-all-start = ((bf16[64,2,256]{2,1,0:T(2,128)(2,1)}), bf16[64,2,256]{2,1,0:T(2,128)(2,1)S(1)}, u32[]{:S(2)}, u32[]{:S(2)}) async-start(bf16[64,2,256]{2,1,0:T(2,128)(2,1)} %all_to_all.6), calls=%async_computation | async-start | bytes 131072 | tf_op jit(solution)/shard_map/all_to_all | solution.py:123
Sparse Core Ops, SparseCore 0:
  11.1 81.0 all-reduce.1
where the time goes:
time: 142 us; the launch traced here: 141 us
  waiting for transfers between devices  79.8 us (56%)
  starting transfers between devices  23.6 us (17%)
  between operations  14.4 us (10%)
  local copies, waits for them, and re-layouts  8.42 us (6%)
  loops' own time  8.37 us (6%)
  matrix products  4.61 us (3%)
  other arithmetic  2.13 us (2%)
    psum x1, waiting for transfers between devices, local(): summed = lax.psum(partial_value, 'tp')  79.8 us
    ppermute x3, starting transfers between devices, shifted(): lax.ppermute(value, axis, [(source, source + steps) for source in range(f...  13.7 us
    all_to_all x1, starting transfers between devices, local(): lax.all_to_all(outgoing, 'req', split_axis=0, concat_axis=0, tiled=True)  9.92 us
    another operation x1, loops' own time, local(): outputs = lax.map(attend_head, jnp.arange(local_heads, dtype=jnp.int32))  8.37 us
    unnamed x12, local copies, waits for them, and re-layouts  2.86 us
  transfers between devices with their start and end apart: 5, of which 1 were waited for; matrix products, arithmetic and copies ran while one was open for 6% of the time, Pallas kernels for 0%

commit v1 on v0

--- a/solution.py
+++ b/solution.py
@@ -33,15 +33,6 @@
     )
 
 
-def rotate_keys(block, positions):
-    rows = block.shape[0]
-    parts = block.shape[1] // HD
-    shaped = block.reshape(rows, parts, HD)
-    turned = rotate(shaped, positions)
-    is_key = jnp.arange(parts, dtype=jnp.int32) % 2 == 0
-    return jnp.where(is_key[None, :, None], turned, shaped).reshape(rows, parts * HD)
-
-
 def segment_info(lengths, indices):
     ends = jnp.cumsum(lengths)
     before = ends[None, :] <= indices[:, None]
@@ -52,22 +43,21 @@
 
 def local(tokens, kv_weight, queries, lengths, page_owner):
     rows = tokens.shape[0]
-    columns = kv_weight.shape[1]
-    share = columns // lax.axis_size("tp")
+    tp_size = lax.axis_size("tp")
     tp_index = lax.axis_index("tp")
     req_index = lax.axis_index("req")
     local_index = req_index * rows + jnp.arange(rows, dtype=jnp.int32)
     segment, positions = segment_info(lengths, local_index)
     local_heads = queries.shape[1] // HD
-    group = HQ // KVH
-    per_group = min(local_heads, group)
-    kv_count = local_heads // per_group
-    first_head = tp_index * local_heads // group
     partial_value = jnp.dot(tokens, kv_weight, preferred_element_type=jnp.float32)
-    summed = lax.psum(partial_value, "tp")
-    cache_rows = rotate_keys(summed, positions).astype(jnp.bfloat16)
-    mine = lax.dynamic_slice_in_dim(cache_rows, tp_index * share, share, 1)
-    near = lax.dynamic_slice_in_dim(cache_rows, first_head * 2 * HD, kv_count * 2 * HD, 1)
+    own = lax.psum_scatter(partial_value, "tp", scatter_dimension=1, tiled=True)
+    is_key = tp_index % 2 == 0
+    turned = rotate(own.reshape(rows, 1, HD), positions).reshape(rows, HD)
+    mine = jnp.where(is_key, turned, own).astype(jnp.bfloat16)
+    other = lax.ppermute(mine, "tp", [(i, i ^ 1) for i in range(tp_size)])
+    key_now = jnp.where(is_key, mine, other)
+    value_now = jnp.where(is_key, other, mine)
+    near = jnp.concatenate([key_now, value_now], axis=1)
     rotated = rotate(queries.astype(jnp.float32).reshape(rows, local_heads, HD), positions).astype(
         jnp.bfloat16
     )
@@ -84,30 +74,23 @@
         & (key_index[None, :] <= local_index[:, None])
         & (key_segment[None, :] == segment[:, None])
     )
-    key_parts = window.reshape(key_total, kv_count, 2, HD)
-    head_keys = jnp.transpose(key_parts[:, :, 0, :], (1, 0, 2))
-    head_values = jnp.transpose(key_parts[:, :, 1, :], (1, 0, 2))
+    key_head = window[:, :HD]
+    value_head = window[:, HD:]
     query_heads = jnp.transpose(rotated, (1, 0, 2))
-
-    def attend_head(head):
-        query_head = query_heads[head]
-        slot = head // per_group
-        key_head = head_keys[slot]
-        value_head = head_values[slot]
-        scores = lax.dot_general(
-            query_head, key_head, (((1,), (1,)), ((), ())), preferred_element_type=jnp.float32
-        ) / math.sqrt(HD)
-        scores = jnp.where(allowed, scores, -1e30)
-        largest = jnp.max(scores, axis=1, keepdims=True)
-        weights = jnp.exp(scores - largest)
-        total = jnp.sum(weights, axis=1, keepdims=True)
-        mixed = jnp.dot(
-            weights.astype(jnp.bfloat16), value_head, preferred_element_type=jnp.float32
-        )
-        return (mixed / total).astype(jnp.bfloat16)
-
-    outputs = lax.map(attend_head, jnp.arange(local_heads, dtype=jnp.int32))
+    scores = lax.dot_general(
+        query_heads, key_head, (((2,), (1,)), ((), ())), preferred_element_type=jnp.float32
+    ) / math.sqrt(HD)
+    scores = jnp.where(allowed[None], scores, -1e30)
+    largest = jnp.max(scores, axis=2, keepdims=True)
+    weights = jnp.exp(scores - largest)
+    total = jnp.sum(weights, axis=2, keepdims=True)
+    mixed = lax.dot_general(
+        weights.astype(jnp.bfloat16), value_head, (((2,), (0,)), ((), ())),
+        preferred_element_type=jnp.float32,
+    )
+    outputs = (mixed / total).astype(jnp.bfloat16)
     attended = jnp.transpose(outputs, (1, 0, 2)).reshape(rows, local_heads * HD)
+    share = mine.shape[1]
     pages_here = page_owner.shape[0]
     owners = page_owner[:, 0]
     page_rows = rows // pages_here

time: 142 us -> 103 us (0.73)
  waiting for transfers between devices: 79.8 us -> 49.7 us
  loops' own time: 8.37 us -> 0 us
  starting transfers between devices: 23.6 us -> 28.4 us
  local copies, waits for them, and re-layouts: 8.42 us -> 4.15 us
    psum x1 -> x0, waiting for transfers between devices: 79.8 us -> none  [local(): summed = lax.psum(partial_value, 'tp')]
    reduce_scatter x0 -> x1, waiting for transfers between devices: none -> 40.2 us  [local(): own = lax.psum_scatter(partial_value, 'tp', scatter_dimension=1, tiled=True)]
    another operation x1 -> x0, loops' own time: 8.37 us -> none  [local(): outputs = lax.map(attend_head, jnp.arange(local_heads, dtype=jnp.int32))]
    all_to_all x1, waiting for transfers between devices: 0.01 us -> 7.99 us  [local(): lax.all_to_all(outgoing, 'req', split_axis=0, concat_axis=0, tiled=True)]
    ppermute x0 -> x1, starting transfers between devices: none -> 3.13 us  [local(): other = lax.ppermute(mine, 'tp', [(i, i ^ 1) for i in range(tp_size)])]
    dynamic_slice x6 -> x0, local copies, waits for them, and re-layouts: 2.7 us -> none  [the longest x4 2.67 us: local(): outputs = lax.map(attend_head, jnp.arange(local_heads, dtype=jnp.int32))]
    ppermute x3, starting transfers between devices: 13.7 us -> 15.3 us  [shifted(): lax.ppermute(value, axis, [(source, source + steps) for source in range(f...]
    ppermute x0 -> x1, waiting for transfers between devices: none -> 1.48 us  [local(): other = lax.ppermute(mine, 'tp', [(i, i ^ 1) for i in range(tp_size)])]
  transfers between devices with their start and end apart: 5 -> 6, of which waited for: 1 -> 3; matrix products, arithmetic and copies ran while one was open for 6% -> 4% of each run, Pallas kernels for 0% -> 0%
where the time goes in v1:
time: 103 us
  waiting for transfers between devices  49.7 us (48%)
  starting transfers between devices  28.4 us (28%)
  between operations  14.3 us (14%)
  local copies, waits for them, and re-layouts  4.15 us (4%)
  matrix products  3.24 us (3%)
  other arithmetic  2.8 us (3%)
    reduce_scatter x1, waiting for transfers between devices, local(): own = lax.psum_scatter(partial_value, 'tp', scatter_dimension=1, tiled=True)  40.2 us
    ppermute x3, starting transfers between devices, shifted(): lax.ppermute(value, axis, [(source, source + steps) for source in range(f...  15.3 us
    all_to_all x1, starting transfers between devices, local(): lax.all_to_all(outgoing, 'req', split_axis=0, concat_axis=0, tiled=True)  9.93 us
    all_to_all x1, waiting for transfers between devices, local(): lax.all_to_all(outgoing, 'req', split_axis=0, concat_axis=0, tiled=True)  7.99 us
    ppermute x1, starting transfers between devices, local(): other = lax.ppermute(mine, 'tp', [(i, i ^ 1) for i in range(tp_size)])  3.13 us
    unnamed x12, local copies, waits for them, and re-layouts  2.67 us
    dot_general x1, matrix products, local(): jnp.dot(tokens, kv_weight, preferred_element_type=jnp.float32)  2.19 us
  transfers between devices with their start and end apart: 6, of which 3 were waited for; matrix products, arithmetic and copies ran while one was open for 4% of the time, Pallas kernels for 0%

profile of v1, /device:TPU:1, one launch (start us, length us, event | category | flops | bytes accessed | tf_op | source)
XLA Modules:
  0.0 102.6 jit_solution(16038006374735601538)
XLA Ops:
  7.2 0.0 copy-start
  7.2 0.0 copy-start.2
  7.2 0.0 copy-start.1
  7.2 0.0 copy-start.3
  7.2 0.0 reduce-scatter.2.cloned.1.call-start
  7.3 1.5 %copy-done = bf16[1024,1024]{1,0:T(8,128)(2,1)S(1)} copy-done((bf16[1024,1024]{1,0:T(8,128)(2,1)S(1)}, bf16[1024,1024]{1,0:T(8,128)(2,1)}, u32[]{:S(2)}) %copy-start) | copy-done | bytes 2097176
  8.8 2.2 %fusion.24 = f32[128,1024]{1,0:T(8,128)} fusion(bf16[128,1024]{1,0:T(8,128)(2,1)} %param.5, bf16[1024,1024]{1,0:T(8,128)(2,1)S(1)} %copy-done), kind=kOutput, calls=%fused_computation.54 | convolution fusion | flops 268435456 | bytes 2883584 | tf_op jit(solution)/shard_map/dot_general | solution.py:52
  11.0 0.0 reduce-scatter.2.cloned.1.call-update
  11.0 0.0 copy-done.2
  11.0 0.1 copy.16
  11.1 0.1 reduce-window.8
  11.2 0.1 reduce
  11.3 0.0 copy-done.1
  11.3 0.1 copy.17
  11.5 0.0 copy-done.3
  11.5 0.2 convert_reduce_fusion.1
  11.6 0.1 convert_reduce_fusion
  11.8 0.1 copy.24
  11.9 0.1 copy.25
  12.0 0.1 fusion.20
  12.1 0.1 compare_and_fusion
  12.3 0.3 multiply_cosine_fusion.1
  12.6 0.1 subtract_convert_fusion
  12.7 40.2 %reduce-scatter.2.cloned.1.call-done = f32[128,128]{1,0:T(8,128)} async-done(((f32[128,1024]{1,0:T(8,128)}), f32[128,128]{1,0:T(8,128)}) %reduce-scatter.2.cloned.1.call-update) | async-done | bytes 65552 | tf_op jit(solution)/shard_map/reduce_scatter | solution.py:53
  52.9 1.2 %fusion.13 = (bf16[128,1,64]{2,0,1:T(8,128)(2,1)S(1)}, bf16[128,1,64]{2,0,1:T(8,128)(2,1)S(1)}) fusion(f32[128,1,128]{2,0,1:T(8,128)} %bitcast.37, f32[64]{0:T(128)S(1)} %multiply_power_fusion, f32[128]{0:T(128)S(1)} %subtract_convert_fusion.1), kind=kLoop, calls=%fused_computation.27 | loop fusion | flops 73728 | bytes 99072 | tf_op jit(solution)/shard_map/sub | solution.py:32
  54.1 0.1 fusion.16
  54.2 3.1 %collective-permute-start = (bf16[128,128]{1,0:T(8,128)(2,1)S(1)}, bf16[128,128]{1,0:T(8,128)(2,1)S(1)}, u32[]{:S(2)}, u32[]{:S(2)}) collective-permute-start(bf16[128,128]{1,0:T(8,128)(2,1)S(1)} %fusion.16), channel_id=1, source_target_pairs={{0,1},{1,0},{2,3},{3,2},{4,5},{5,4},{6,7},{7,6},{8,9},{9,8},{10,11... | collective-permute-start | bytes 98312 | tf_op jit(solution)/shard_map/ppermute | solution.py:57
  57.4 1.5 %collective-permute-done = bf16[128,128]{1,0:T(8,128)(2,1)S(1)} collective-permute-done((bf16[128,128]{1,0:T(8,128)(2,1)S(1)}, bf16[128,128]{1,0:T(8,128)(2,1)S(1)}, u32[]{:S(2)}, u32[]{:S(2)}) %collective-permute-start) | collective-permute-done | bytes 32800 | tf_op jit(solution)/shard_map/ppermute | solution.py:57
  58.9 11.2 %collective-permute-start.1 = (bf16[128,256]{1,0:T(8,128)(2,1)S(1)}, bf16[128,256]{1,0:T(8,128)(2,1)S(1)}, u32[]{:S(2)}, u32[]{:S(2)}) collective-permute-start(bf16[128,256]{1,0:T(8,128)(2,1)S(1)} %pad_maximum_fusion), channel_id=1, source_target_pairs={{0,24},{8,32},{16,40},{24,48},{32,56},{40,64},{48,72},{56,80},{64,... | collective-permute-start | bytes 196616 | tf_op jit(solution)/shard_map/ppermute | solution.py:20
  70.1 2.2 %collective-permute-start.2 = (bf16[128,256]{1,0:T(8,128)(2,1)S(1)}, bf16[128,256]{1,0:T(8,128)(2,1)S(1)}, u32[]{:S(2)}, u32[]{:S(2)}) collective-permute-start(bf16[128,256]{1,0:T(8,128)(2,1)S(1)} %pad_maximum_fusion), channel_id=1, source_target_pairs={{0,16},{8,24},{16,32},{24,40},{32,48},{40,56},{48,64},{56,72},{64,... | collective-permute-start | bytes 196616 | tf_op jit(solution)/shard_map/ppermute | solution.py:20
  72.3 1.9 %collective-permute-start.3 = (bf16[128,256]{1,0:T(8,128)(2,1)S(1)}, bf16[128,256]{1,0:T(8,128)(2,1)S(1)}, u32[]{:S(2)}, u32[]{:S(2)}) collective-permute-start(bf16[128,256]{1,0:T(8,128)(2,1)S(1)} %pad_maximum_fusion), channel_id=1, source_target_pairs={{0,8},{8,16},{16,24},{24,32},{32,40},{40,48},{48,56},{56,64},{64,7... | collective-permute-start | bytes 196616 | tf_op jit(solution)/shard_map/ppermute | solution.py:20
  74.3 0.1 convolution_convert_fusion
  74.4 0.7 all_to_all.6
  75.1 9.9 %all-to-all-start = ((bf16[64,2,256]{2,1,0:T(2,128)(2,1)}), bf16[64,2,256]{2,1,0:T(2,128)(2,1)S(1)}, u32[]{:S(2)}, u32[]{:S(2)}) async-start(bf16[64,2,256]{2,1,0:T(2,128)(2,1)} %all_to_all.6), calls=%async_computation.1 | async-start | bytes 131072 | tf_op jit(solution)/shard_map/all_to_all | solution.py:106
  85.0 0.0 collective-permute-done.1
  85.0 0.0 collective-permute-done.2
  85.0 0.0 collective-permute-done.3
  85.1 0.5 fusion.23
  85.5 0.3 fusion.3
  85.9 0.5 fusion.2
  86.3 0.8 copy.21
  87.1 8.0 %all-to-all-done = bf16[64,2,256]{2,1,0:T(2,128)(2,1)S(1)} async-done(((bf16[64,2,256]{2,1,0:T(2,128)(2,1)}), bf16[64,2,256]{2,1,0:T(2,128)(2,1)S(1)}, u32[]{:S(2)}, u32[]{:S(2)}) %all-to-all-start) | async-done | bytes 65568 | tf_op jit(solution)/shard_map/all_to_all | solution.py:106
  95.1 0.7 reshape.264
  (11 shorter events, 0.1 us)
Async XLA Ops:
  7.2 1.6 %copy-start = (bf16[1024,1024]{1,0:T(8,128)(2,1)S(1)}, bf16[1024,1024]{1,0:T(8,128)(2,1)}, u32[]{:S(2)}) copy-start(bf16[1024,1024]{1,0:T(8,128)(2,1)} %param.6) | copy-start | bytes 6291460
  7.2 3.8 %copy-start.2 = (s32[32]{0:T(128)S(1)}, s32[32]{0:T(128)}, u32[]{:S(2)}) copy-start(s32[32]{0:T(128)} %param.8) | copy-start | bytes 388
  7.2 4.1 %copy-start.1 = (bf16[128,512]{1,0:T(8,128)(2,1)S(1)}, bf16[128,512]{1,0:T(8,128)(2,1)}, u32[]{:S(2)}) copy-start(bf16[128,512]{1,0:T(8,128)(2,1)} %param.7) | copy-start | bytes 393220
  7.2 4.3 %copy-start.3 = (s32[64,1]{0,1:T(1,128)S(1)}, s32[64,1]{0,1:T(1,128)}, u32[]{:S(2)}) copy-start(s32[64,1]{0,1:T(1,128)} %param.9) | copy-start | bytes 772
  7.2 45.7 %reduce-scatter.2.cloned.1.call-start = ((), (), s32[]{:S(2)}) async-start(), calls=%async_computation.2 | async-start | bytes 589824 | tf_op jit(solution)/shard_map/reduce_scatter | solution.py:53
  54.2 4.7 %collective-permute-start = (bf16[128,128]{1,0:T(8,128)(2,1)S(1)}, bf16[128,128]{1,0:T(8,128)(2,1)S(1)}, u32[]{:S(2)}, u32[]{:S(2)}) collective-permute-start(bf16[128,128]{1,0:T(8,128)(2,1)S(1)} %fusion.16), channel_id=1, source_target_pairs={{0,1},{1,0},{2,3},{3,2},{4,5},{5,4},{6,7},{7,6},{8,9},{9,8},{10,11... | collective-permute-start | bytes 98312 | tf_op jit(solution)/shard_map/ppermute | solution.py:57
  58.9 26.1 %collective-permute-start.1 = (bf16[128,256]{1,0:T(8,128)(2,1)S(1)}, bf16[128,256]{1,0:T(8,128)(2,1)S(1)}, u32[]{:S(2)}, u32[]{:S(2)}) collective-permute-start(bf16[128,256]{1,0:T(8,128)(2,1)S(1)} %pad_maximum_fusion), channel_id=1, source_target_pairs={{0,24},{8,32},{16,40},{24,48},{32,56},{40,64},{48,72},{56,80},{64,... | collective-permute-start | bytes 196616 | tf_op jit(solution)/shard_map/ppermute | solution.py:20
  70.1 14.9 %collective-permute-start.2 = (bf16[128,256]{1,0:T(8,128)(2,1)S(1)}, bf16[128,256]{1,0:T(8,128)(2,1)S(1)}, u32[]{:S(2)}, u32[]{:S(2)}) collective-permute-start(bf16[128,256]{1,0:T(8,128)(2,1)S(1)} %pad_maximum_fusion), channel_id=1, source_target_pairs={{0,16},{8,24},{16,32},{24,40},{32,48},{40,56},{48,64},{56,72},{64,... | collective-permute-start | bytes 196616 | tf_op jit(solution)/shard_map/ppermute | solution.py:20
  72.3 12.7 %collective-permute-start.3 = (bf16[128,256]{1,0:T(8,128)(2,1)S(1)}, bf16[128,256]{1,0:T(8,128)(2,1)S(1)}, u32[]{:S(2)}, u32[]{:S(2)}) collective-permute-start(bf16[128,256]{1,0:T(8,128)(2,1)S(1)} %pad_maximum_fusion), channel_id=1, source_target_pairs={{0,8},{8,16},{16,24},{24,32},{32,40},{40,48},{48,56},{56,64},{64,7... | collective-permute-start | bytes 196616 | tf_op jit(solution)/shard_map/ppermute | solution.py:20
  75.1 20.0 %all-to-all-start = ((bf16[64,2,256]{2,1,0:T(2,128)(2,1)}), bf16[64,2,256]{2,1,0:T(2,128)(2,1)S(1)}, u32[]{:S(2)}, u32[]{:S(2)}) async-start(bf16[64,2,256]{2,1,0:T(2,128)(2,1)} %all_to_all.6), calls=%async_computation.1 | async-start | bytes 131072 | tf_op jit(solution)/shard_map/all_to_all | solution.py:106
Sparse Core Ops, SparseCore 0:
  11.1 41.7 reduce-scatter.1

commit v2 on v1

--- a/solution.py
+++ b/solution.py
@@ -50,14 +50,15 @@
     segment, positions = segment_info(lengths, local_index)
     local_heads = queries.shape[1] // HD
     partial_value = jnp.dot(tokens, kv_weight, preferred_element_type=jnp.float32)
-    own = lax.psum_scatter(partial_value, "tp", scatter_dimension=1, tiled=True)
-    is_key = tp_index % 2 == 0
-    turned = rotate(own.reshape(rows, 1, HD), positions).reshape(rows, HD)
-    mine = jnp.where(is_key, turned, own).astype(jnp.bfloat16)
-    other = lax.ppermute(mine, "tp", [(i, i ^ 1) for i in range(tp_size)])
-    key_now = jnp.where(is_key, mine, other)
-    value_now = jnp.where(is_key, other, mine)
-    near = jnp.concatenate([key_now, value_now], axis=1)
+    heads_here = partial_value.shape[1] // (2 * HD)
+    per_head = tp_size // heads_here
+    pieces = partial_value.astype(jnp.bfloat16).reshape(rows, heads_here, 2 * HD)
+    pieces = jnp.repeat(jnp.transpose(pieces, (1, 0, 2)), per_head, axis=0)
+    arrived = lax.all_to_all(pieces, "tp", 0, 0, tiled=True)
+    head_sum = jnp.sum(arrived.astype(jnp.float32), axis=0)
+    key_now = rotate(head_sum[:, :HD].reshape(rows, 1, HD), positions).reshape(rows, HD)
+    near = jnp.concatenate([key_now, head_sum[:, HD:]], axis=1).astype(jnp.bfloat16)
+    mine = lax.dynamic_slice_in_dim(near, (tp_index % per_head) * HD, HD, 1)
     rotated = rotate(queries.astype(jnp.float32).reshape(rows, local_heads, HD), positions).astype(
         jnp.bfloat16
     )

time: 103 us -> 65.4 us (0.63)
  waiting for transfers between devices: 49.7 us -> 24.2 us
  between operations: 14.3 us -> 0.97 us
  starting transfers between devices: 28.4 us -> 29.9 us
  local copies, waits for them, and re-layouts: 4.15 us -> 5.6 us
    reduce_scatter x1 -> x0, waiting for transfers between devices: 40.2 us -> none  [local(): own = lax.psum_scatter(partial_value, 'tp', scatter_dimension=1, tiled=True)]
    all_to_all x0 -> x1, waiting for transfers between devices: none -> 16.2 us  [local(): arrived = lax.all_to_all(pieces, 'tp', 0, 0, tiled=True)]
    all_to_all x0 -> x1, starting transfers between devices: none -> 10.9 us  [local(): arrived = lax.all_to_all(pieces, 'tp', 0, 0, tiled=True)]
    ppermute x3, starting transfers between devices: 15.3 us -> 10.1 us  [shifted(): lax.ppermute(value, axis, [(source, source + steps) for source in range(f...]
    ppermute x1 -> x0, starting transfers between devices: 3.13 us -> none  [local(): other = lax.ppermute(mine, 'tp', [(i, i ^ 1) for i in range(tp_size)])]
    ppermute x1 -> x0, waiting for transfers between devices: 1.48 us -> none  [local(): other = lax.ppermute(mine, 'tp', [(i, i ^ 1) for i in range(tp_size)])]
    sub x1 -> x0, other arithmetic: 1.23 us -> none  [rotate(): front * cosine - behind * sine]
    unnamed x12 -> x14, local copies, waits for them, and re-layouts: 2.67 us -> 2.96 us
  transfers between devices with their start and end apart: 6 -> 5, of which waited for: 3 -> 2; matrix products, arithmetic and copies ran while one was open for 4% -> 6% of each run, Pallas kernels for 0% -> 0%
where the time goes in v2:
time: 65.4 us; the launch traced here: 65.1 us
  starting transfers between devices  29.9 us (46%)
  waiting for transfers between devices  24.2 us (37%)
  local copies, waits for them, and re-layouts  5.6 us (9%)
  matrix products  2.45 us (4%)
  other arithmetic  1.88 us (3%)
  between operations  0.97 us (1%)
    all_to_all x1, waiting for transfers between devices, local(): arrived = lax.all_to_all(pieces, 'tp', 0, 0, tiled=True)  16.2 us
    all_to_all x1, starting transfers between devices, local(): arrived = lax.all_to_all(pieces, 'tp', 0, 0, tiled=True)  10.9 us
    ppermute x3, starting transfers between devices, shifted(): lax.ppermute(value, axis, [(source, source + steps) for source in range(f...  10.1 us
    all_to_all x1, starting transfers between devices, local(): lax.all_to_all(outgoing, 'req', split_axis=0, concat_axis=0, tiled=True)  9.02 us
    all_to_all x1, waiting for transfers between devices, local(): lax.all_to_all(outgoing, 'req', split_axis=0, concat_axis=0, tiled=True)  7.99 us
    unnamed x14, local copies, waits for them, and re-layouts  2.96 us
    dot_general x1, matrix products, local(): jnp.dot(tokens, kv_weight, preferred_element_type=jnp.float32)  1.39 us
  transfers between devices with their start and end apart: 5, of which 2 were waited for; matrix products, arithmetic and copies ran while one was open for 6% of the time, Pallas kernels for 0%

profile of v2, /device:TPU:1, one launch (start us, length us, event | category | flops | bytes accessed | tf_op | source)
XLA Modules:
  0.0 65.1 jit_solution(13745909946373736521)
XLA Ops:
  0.6 0.0 copy-start
  0.6 1.6 %copy-done = bf16[1024,1024]{1,0:T(8,128)(2,1)S(1)} copy-done((bf16[1024,1024]{1,0:T(8,128)(2,1)S(1)}, bf16[1024,1024]{1,0:T(8,128)(2,1)}, u32[]{:S(2)}) %copy-start) | copy-done | bytes 2097176
  2.2 1.4 %convolution_convert_fusion = bf16[128,1024]{1,0:T(8,128)(2,1)S(1)} fusion(bf16[128,1024]{1,0:T(8,128)(2,1)} %param.5, bf16[1024,1024]{1,0:T(8,128)(2,1)S(1)} %copy-done), kind=kOutput, calls=%fused_computation.2 | convolution fusion | flops 268566528 | bytes 2621440 | tf_op jit(solution)/shard_map/dot_general | solution.py:52
  3.6 0.0 copy-start.3
  3.6 0.0 copy-start.2
  3.7 0.0 copy-start.1
  3.7 0.2 reshape.267
  3.9 0.8 %broadcast_in_dim.25 = bf16[4,2,128,256]{3,2,1,0:T(8,128)(2,1)} broadcast(bf16[4,128,256]{2,1,0:T(8,128)(2,1)S(1)} %copy.38), dimensions={0,2,3} | broadcast | bytes 786432 | tf_op jit(solution)/shard_map/broadcast_in_dim | solution.py:56
  4.7 10.9 %all-to-all-start = ((bf16[8,128,256]{2,1,0:T(8,128)(2,1)}), bf16[8,128,256]{2,1,0:T(8,128)(2,1)S(1)}, u32[]{:S(2)}, u32[]{:S(2)}) async-start(bf16[8,128,256]{2,1,0:T(8,128)(2,1)} %bitcast.5), calls=%async_computation | async-start | bytes 1048576 | tf_op jit(solution)/shard_map/all_to_all | solution.py:57
  15.6 0.0 copy-done.3
  15.6 0.2 convert_reduce_fusion.2
  15.8 0.0 copy-done.2
  15.8 0.1 copy.34
  15.9 0.1 reduce-window.8
  16.0 0.1 reduce
  16.1 0.1 fusion.21
  16.2 0.1 convert_reduce_fusion.1
  16.3 0.0 copy-done.1
  16.3 0.1 copy.35
  16.4 0.1 copy.47
  16.6 0.1 copy.46
  16.7 0.1 compare_and_fusion
  16.9 0.3 multiply_cosine_fusion
  17.2 0.1 subtract_convert_fusion
  17.3 16.2 %all-to-all-done = bf16[8,128,256]{2,1,0:T(8,128)(2,1)S(1)} async-done(((bf16[8,128,256]{2,1,0:T(8,128)(2,1)}), bf16[8,128,256]{2,1,0:T(8,128)(2,1)S(1)}, u32[]{:S(2)}, u32[]{:S(2)}) %all-to-all-start) | async-done | bytes 524320 | tf_op jit(solution)/shard_map/all_to_all | solution.py:57
  33.5 0.1 convert_reduce_fusion
  33.6 0.1 copy.49
  33.7 0.1 copy.48
  33.8 0.2 fusion.14
  34.1 3.5 %collective-permute-start.2 = (bf16[128,256]{0,1:T(8,128)(2,1)S(1)}, bf16[128,256]{0,1:T(8,128)(2,1)S(1)}, u32[]{:S(2)}, u32[]{:S(2)}) collective-permute-start(bf16[128,256]{0,1:T(8,128)(2,1)S(1)} %pad_maximum_fusion), channel_id=1, source_target_pairs={{0,8},{8,16},{16,24},{24,32},{32,40},{40,48},{48,56},{56,64},{64,7... | collective-permute-start | bytes 196616 | tf_op jit(solution)/shard_map/ppermute | solution.py:20
  37.6 3.1 %collective-permute-start.1 = (bf16[128,256]{0,1:T(8,128)(2,1)S(1)}, bf16[128,256]{0,1:T(8,128)(2,1)S(1)}, u32[]{:S(2)}, u32[]{:S(2)}) collective-permute-start(bf16[128,256]{0,1:T(8,128)(2,1)S(1)} %pad_maximum_fusion), channel_id=1, source_target_pairs={{0,16},{8,24},{16,32},{24,40},{32,48},{40,56},{48,64},{56,72},{64,... | collective-permute-start | bytes 196616 | tf_op jit(solution)/shard_map/ppermute | solution.py:20
  40.7 3.4 %collective-permute-start = (bf16[128,256]{0,1:T(8,128)(2,1)S(1)}, bf16[128,256]{0,1:T(8,128)(2,1)S(1)}, u32[]{:S(2)}, u32[]{:S(2)}) collective-permute-start(bf16[128,256]{0,1:T(8,128)(2,1)S(1)} %pad_maximum_fusion), channel_id=1, source_target_pairs={{0,24},{8,32},{16,40},{24,48},{32,56},{40,64},{48,72},{56,80},{64,... | collective-permute-start | bytes 196616 | tf_op jit(solution)/shard_map/ppermute | solution.py:20
  44.2 0.1 fusion.17
  44.3 0.1 copy.42
  44.5 0.1 convolution_convert_fusion.1
  44.6 0.7 %all_to_all.10 = bf16[64,2,256]{2,1,0:T(2,128)(2,1)} reshape(bf16[128,256]{1,0:T(8,128)(2,1)S(1)} %convolution_convert_fusion.1) | data formatting | bytes 131072 | tf_op jit(solution)/shard_map/all_to_all | solution.py:107
  45.3 9.0 %all-to-all-start.1 = ((bf16[64,2,256]{2,1,0:T(2,128)(2,1)}), bf16[64,2,256]{2,1,0:T(2,128)(2,1)S(1)}, u32[]{:S(2)}, u32[]{:S(2)}) async-start(bf16[64,2,256]{2,1,0:T(2,128)(2,1)} %all_to_all.10), calls=%async_computation.1 | async-start | bytes 131072 | tf_op jit(solution)/shard_map/all_to_all | solution.py:107
  54.3 0.0 collective-permute-done.2
  54.3 0.0 collective-permute-done.1
  54.3 0.0 collective-permute-done
  54.4 0.5 fusion.24
  54.8 0.3 fusion.3
  55.2 0.5 fusion.2
  55.6 0.8 %copy.43 = bf16[128,512]{1,0:T(8,128)(2,1)} copy(bf16[128,512]{0,1:T(8,128)(2,1)S(1)} %bitcast.37) | data formatting | bytes 262144
  56.4 8.0 %all-to-all-done.1 = bf16[64,2,256]{2,1,0:T(2,128)(2,1)S(1)} async-done(((bf16[64,2,256]{2,1,0:T(2,128)(2,1)}), bf16[64,2,256]{2,1,0:T(2,128)(2,1)S(1)}, u32[]{:S(2)}, u32[]{:S(2)}) %all-to-all-start.1) | async-done | bytes 65568 | tf_op jit(solution)/shard_map/all_to_all | solution.py:107
  64.4 0.7 %reshape.273 = bf16[256,128]{1,0:T(8,128)(2,1)} reshape(bf16[64,2,256]{2,1,0:T(2,128)(2,1)S(1)} %all-to-all-done.1) | data formatting | bytes 131072 | tf_op jit(solution)/shard_map/reshape | solution.py:108
  (14 shorter events, 0.2 us)
Async XLA Ops:
  0.6 1.6 %copy-start = (bf16[1024,1024]{1,0:T(8,128)(2,1)S(1)}, bf16[1024,1024]{1,0:T(8,128)(2,1)}, u32[]{:S(2)}) copy-start(bf16[1024,1024]{1,0:T(8,128)(2,1)} %param.6) | copy-start | bytes 6291460
  3.6 12.0 %copy-start.3 = (s32[64,1]{0,1:T(1,128)S(1)}, s32[64,1]{0,1:T(1,128)}, u32[]{:S(2)}) copy-start(s32[64,1]{0,1:T(1,128)} %param.9) | copy-start | bytes 772
  3.6 12.2 %copy-start.2 = (s32[32]{0:T(128)S(1)}, s32[32]{0:T(128)}, u32[]{:S(2)}) copy-start(s32[32]{0:T(128)} %param.8) | copy-start | bytes 388
  3.7 12.6 %copy-start.1 = (bf16[128,512]{1,0:T(8,128)(2,1)S(1)}, bf16[128,512]{1,0:T(8,128)(2,1)}, u32[]{:S(2)}) copy-start(bf16[128,512]{1,0:T(8,128)(2,1)} %param.7) | copy-start | bytes 393220
  4.7 28.8 %all-to-all-start = ((bf16[8,128,256]{2,1,0:T(8,128)(2,1)}), bf16[8,128,256]{2,1,0:T(8,128)(2,1)S(1)}, u32[]{:S(2)}, u32[]{:S(2)}) async-start(bf16[8,128,256]{2,1,0:T(8,128)(2,1)} %bitcast.5), calls=%async_computation | async-start | bytes 1048576 | tf_op jit(solution)/shard_map/all_to_all | solution.py:57
  34.1 20.2 %collective-permute-start.2 = (bf16[128,256]{0,1:T(8,128)(2,1)S(1)}, bf16[128,256]{0,1:T(8,128)(2,1)S(1)}, u32[]{:S(2)}, u32[]{:S(2)}) collective-permute-start(bf16[128,256]{0,1:T(8,128)(2,1)S(1)} %pad_maximum_fusion), channel_id=1, source_target_pairs={{0,8},{8,16},{16,24},{24,32},{32,40},{40,48},{48,56},{56,64},{64,7... | collective-permute-start | bytes 196616 | tf_op jit(solution)/shard_map/ppermute | solution.py:20
  37.6 16.7 %collective-permute-start.1 = (bf16[128,256]{0,1:T(8,128)(2,1)S(1)}, bf16[128,256]{0,1:T(8,128)(2,1)S(1)}, u32[]{:S(2)}, u32[]{:S(2)}) collective-permute-start(bf16[128,256]{0,1:T(8,128)(2,1)S(1)} %pad_maximum_fusion), channel_id=1, source_target_pairs={{0,16},{8,24},{16,32},{24,40},{32,48},{40,56},{48,64},{56,72},{64,... | collective-permute-start | bytes 196616 | tf_op jit(solution)/shard_map/ppermute | solution.py:20
  40.7 13.6 %collective-permute-start = (bf16[128,256]{0,1:T(8,128)(2,1)S(1)}, bf16[128,256]{0,1:T(8,128)(2,1)S(1)}, u32[]{:S(2)}, u32[]{:S(2)}) collective-permute-start(bf16[128,256]{0,1:T(8,128)(2,1)S(1)} %pad_maximum_fusion), channel_id=1, source_target_pairs={{0,24},{8,32},{16,40},{24,48},{32,56},{40,64},{48,72},{56,80},{64,... | collective-permute-start | bytes 196616 | tf_op jit(solution)/shard_map/ppermute | solution.py:20
  45.3 19.1 %all-to-all-start.1 = ((bf16[64,2,256]{2,1,0:T(2,128)(2,1)}), bf16[64,2,256]{2,1,0:T(2,128)(2,1)S(1)}, u32[]{:S(2)}, u32[]{:S(2)}) async-start(bf16[64,2,256]{2,1,0:T(2,128)(2,1)} %all_to_all.10), calls=%async_computation.1 | async-start | bytes 131072 | tf_op jit(solution)/shard_map/all_to_all | solution.py:107

commit v3 on v2

--- a/solution.py
+++ b/solution.py
@@ -5,9 +5,8 @@
 from jax import lax
 from jax.sharding import PartitionSpec as P
 
+
 HD = 128
-HQ = 32
-KVH = 4
 BACK = 3
 
 
@@ -41,7 +40,7 @@
     return (segment, indices - start)
 
 
-def local(tokens, kv_weight, queries, lengths, page_owner):
+def layer(tokens, kv_weight, queries, lengths, page_owner):
     rows = tokens.shape[0]
     tp_size = lax.axis_size("tp")
     tp_index = lax.axis_index("tp")
@@ -69,7 +68,7 @@
     window = jnp.concatenate(blocks, axis=0)
     key_total = (BACK + 1) * rows
     key_index = (req_index - BACK) * rows + jnp.arange(key_total, dtype=jnp.int32)
-    key_segment, unused = segment_info(lengths, key_index)
+    key_segment, _ = segment_info(lengths, key_index)
     allowed = (
         (key_index[None, :] >= 0)
         & (key_index[None, :] <= local_index[:, None])
@@ -112,4 +111,4 @@
 def solution(mesh):
     in_specs = (P("req", "tp"), P("tp", None), P("req", "tp"), P(), P("req", None))
     out_specs = (P("req", "tp"), P("req", "tp"))
-    return jax.shard_map(local, mesh=mesh, in_specs=in_specs, out_specs=out_specs, check_vma=False)
+    return jax.shard_map(layer, mesh=mesh, in_specs=in_specs, out_specs=out_specs, check_vma=False)

time: 65.4 us -> 65.4 us (level)
  no operation moved by 1% of the time
where the time goes in v3:
time: 65.4 us; the launch traced here: 65.1 us
  starting transfers between devices  29.9 us (46%)
  waiting for transfers between devices  24.2 us (37%)
  local copies, waits for them, and re-layouts  5.6 us (9%)
  matrix products  2.45 us (4%)
  other arithmetic  1.88 us (3%)
  between operations  0.97 us (1%)
    all_to_all x1, waiting for transfers between devices, layer(): arrived = lax.all_to_all(pieces, 'tp', 0, 0, tiled=True)  16.2 us
    all_to_all x1, starting transfers between devices, layer(): arrived = lax.all_to_all(pieces, 'tp', 0, 0, tiled=True)  10.9 us
    ppermute x3, starting transfers between devices, shifted(): lax.ppermute(value, axis, [(source, source + steps) for source in range(f...  10.1 us
    all_to_all x1, starting transfers between devices, layer(): lax.all_to_all(outgoing, 'req', split_axis=0, concat_axis=0, tiled=True)  9.02 us
    all_to_all x1, waiting for transfers between devices, layer(): lax.all_to_all(outgoing, 'req', split_axis=0, concat_axis=0, tiled=True)  7.99 us
    unnamed x14, local copies, waits for them, and re-layouts  2.96 us
    dot_general x1, matrix products, layer(): jnp.dot(tokens, kv_weight, preferred_element_type=jnp.float32)  1.39 us
  transfers between devices with their start and end apart: 5, of which 2 were waited for; matrix products, arithmetic and copies ran while one was open for 6% of the time, Pallas kernels for 0%

profile of v3, /device:TPU:1, one launch (start us, length us, event | category | flops | bytes accessed | tf_op | source)
XLA Modules:
  0.0 65.1 jit_solution(13745909946373736521)
XLA Ops:
  0.6 0.0 copy-start
  0.6 1.6 %copy-done = bf16[1024,1024]{1,0:T(8,128)(2,1)S(1)} copy-done((bf16[1024,1024]{1,0:T(8,128)(2,1)S(1)}, bf16[1024,1024]{1,0:T(8,128)(2,1)}, u32[]{:S(2)}) %copy-start) | copy-done | bytes 2097176
  2.2 1.4 %convolution_convert_fusion = bf16[128,1024]{1,0:T(8,128)(2,1)S(1)} fusion(bf16[128,1024]{1,0:T(8,128)(2,1)} %param.5, bf16[1024,1024]{1,0:T(8,128)(2,1)S(1)} %copy-done), kind=kOutput, calls=%fused_computation.2 | convolution fusion | flops 268566528 | bytes 2621440 | tf_op jit(solution)/shard_map/dot_general | solution.py:51
  3.6 0.0 copy-start.3
  3.6 0.0 copy-start.2
  3.7 0.0 copy-start.1
  3.7 0.2 reshape.267
  3.9 0.8 %broadcast_in_dim.25 = bf16[4,2,128,256]{3,2,1,0:T(8,128)(2,1)} broadcast(bf16[4,128,256]{2,1,0:T(8,128)(2,1)S(1)} %copy.38), dimensions={0,2,3} | broadcast | bytes 786432 | tf_op jit(solution)/shard_map/broadcast_in_dim | solution.py:55
  4.7 10.9 %all-to-all-start = ((bf16[8,128,256]{2,1,0:T(8,128)(2,1)}), bf16[8,128,256]{2,1,0:T(8,128)(2,1)S(1)}, u32[]{:S(2)}, u32[]{:S(2)}) async-start(bf16[8,128,256]{2,1,0:T(8,128)(2,1)} %bitcast.5), calls=%async_computation | async-start | bytes 1048576 | tf_op jit(solution)/shard_map/all_to_all | solution.py:56
  15.6 0.0 copy-done.3
  15.6 0.2 convert_reduce_fusion.2
  15.8 0.0 copy-done.2
  15.8 0.1 copy.34
  15.9 0.1 reduce-window.8
  16.0 0.1 reduce
  16.1 0.1 fusion.21
  16.2 0.1 convert_reduce_fusion.1
  16.3 0.0 copy-done.1
  16.3 0.1 copy.35
  16.4 0.1 copy.47
  16.6 0.1 copy.46
  16.7 0.1 compare_and_fusion
  16.9 0.3 multiply_cosine_fusion
  17.2 0.1 subtract_convert_fusion
  17.3 16.2 %all-to-all-done = bf16[8,128,256]{2,1,0:T(8,128)(2,1)S(1)} async-done(((bf16[8,128,256]{2,1,0:T(8,128)(2,1)}), bf16[8,128,256]{2,1,0:T(8,128)(2,1)S(1)}, u32[]{:S(2)}, u32[]{:S(2)}) %all-to-all-start) | async-done | bytes 524320 | tf_op jit(solution)/shard_map/all_to_all | solution.py:56
  33.5 0.1 convert_reduce_fusion
  33.6 0.1 copy.49
  33.7 0.1 copy.48
  33.8 0.2 fusion.14
  34.1 3.5 %collective-permute-start.2 = (bf16[128,256]{0,1:T(8,128)(2,1)S(1)}, bf16[128,256]{0,1:T(8,128)(2,1)S(1)}, u32[]{:S(2)}, u32[]{:S(2)}) collective-permute-start(bf16[128,256]{0,1:T(8,128)(2,1)S(1)} %pad_maximum_fusion), channel_id=1, source_target_pairs={{0,8},{8,16},{16,24},{24,32},{32,40},{40,48},{48,56},{56,64},{64,7... | collective-permute-start | bytes 196616 | tf_op jit(solution)/shard_map/ppermute | solution.py:19
  37.6 3.1 %collective-permute-start.1 = (bf16[128,256]{0,1:T(8,128)(2,1)S(1)}, bf16[128,256]{0,1:T(8,128)(2,1)S(1)}, u32[]{:S(2)}, u32[]{:S(2)}) collective-permute-start(bf16[128,256]{0,1:T(8,128)(2,1)S(1)} %pad_maximum_fusion), channel_id=1, source_target_pairs={{0,16},{8,24},{16,32},{24,40},{32,48},{40,56},{48,64},{56,72},{64,... | collective-permute-start | bytes 196616 | tf_op jit(solution)/shard_map/ppermute | solution.py:19
  40.7 3.4 %collective-permute-start = (bf16[128,256]{0,1:T(8,128)(2,1)S(1)}, bf16[128,256]{0,1:T(8,128)(2,1)S(1)}, u32[]{:S(2)}, u32[]{:S(2)}) collective-permute-start(bf16[128,256]{0,1:T(8,128)(2,1)S(1)} %pad_maximum_fusion), channel_id=1, source_target_pairs={{0,24},{8,32},{16,40},{24,48},{32,56},{40,64},{48,72},{56,80},{64,... | collective-permute-start | bytes 196616 | tf_op jit(solution)/shard_map/ppermute | solution.py:19
  44.2 0.1 fusion.17
  44.3 0.1 copy.42
  44.5 0.1 convolution_convert_fusion.1
  44.6 0.7 %all_to_all.10 = bf16[64,2,256]{2,1,0:T(2,128)(2,1)} reshape(bf16[128,256]{1,0:T(8,128)(2,1)S(1)} %convolution_convert_fusion.1) | data formatting | bytes 131072 | tf_op jit(solution)/shard_map/all_to_all | solution.py:106
  45.3 9.0 %all-to-all-start.1 = ((bf16[64,2,256]{2,1,0:T(2,128)(2,1)}), bf16[64,2,256]{2,1,0:T(2,128)(2,1)S(1)}, u32[]{:S(2)}, u32[]{:S(2)}) async-start(bf16[64,2,256]{2,1,0:T(2,128)(2,1)} %all_to_all.10), calls=%async_computation.1 | async-start | bytes 131072 | tf_op jit(solution)/shard_map/all_to_all | solution.py:106
  54.3 0.0 collective-permute-done.2
  54.3 0.0 collective-permute-done.1
  54.3 0.0 collective-permute-done
  54.4 0.5 fusion.24
  54.8 0.3 fusion.3
  55.2 0.5 fusion.2
  55.6 0.8 %copy.43 = bf16[128,512]{1,0:T(8,128)(2,1)} copy(bf16[128,512]{0,1:T(8,128)(2,1)S(1)} %bitcast.37) | data formatting | bytes 262144
  56.4 8.0 %all-to-all-done.1 = bf16[64,2,256]{2,1,0:T(2,128)(2,1)S(1)} async-done(((bf16[64,2,256]{2,1,0:T(2,128)(2,1)}), bf16[64,2,256]{2,1,0:T(2,128)(2,1)S(1)}, u32[]{:S(2)}, u32[]{:S(2)}) %all-to-all-start.1) | async-done | bytes 65568 | tf_op jit(solution)/shard_map/all_to_all | solution.py:106
  64.4 0.7 %reshape.273 = bf16[256,128]{1,0:T(8,128)(2,1)} reshape(bf16[64,2,256]{2,1,0:T(2,128)(2,1)S(1)} %all-to-all-done.1) | data formatting | bytes 131072 | tf_op jit(solution)/shard_map/reshape | solution.py:107
  (14 shorter events, 0.2 us)
Async XLA Ops:
  0.6 1.6 %copy-start = (bf16[1024,1024]{1,0:T(8,128)(2,1)S(1)}, bf16[1024,1024]{1,0:T(8,128)(2,1)}, u32[]{:S(2)}) copy-start(bf16[1024,1024]{1,0:T(8,128)(2,1)} %param.6) | copy-start | bytes 6291460
  3.6 12.0 %copy-start.3 = (s32[64,1]{0,1:T(1,128)S(1)}, s32[64,1]{0,1:T(1,128)}, u32[]{:S(2)}) copy-start(s32[64,1]{0,1:T(1,128)} %param.9) | copy-start | bytes 772
  3.6 12.2 %copy-start.2 = (s32[32]{0:T(128)S(1)}, s32[32]{0:T(128)}, u32[]{:S(2)}) copy-start(s32[32]{0:T(128)} %param.8) | copy-start | bytes 388
  3.7 12.6 %copy-start.1 = (bf16[128,512]{1,0:T(8,128)(2,1)S(1)}, bf16[128,512]{1,0:T(8,128)(2,1)}, u32[]{:S(2)}) copy-start(bf16[128,512]{1,0:T(8,128)(2,1)} %param.7) | copy-start | bytes 393220
  4.7 28.8 %all-to-all-start = ((bf16[8,128,256]{2,1,0:T(8,128)(2,1)}), bf16[8,128,256]{2,1,0:T(8,128)(2,1)S(1)}, u32[]{:S(2)}, u32[]{:S(2)}) async-start(bf16[8,128,256]{2,1,0:T(8,128)(2,1)} %bitcast.5), calls=%async_computation | async-start | bytes 1048576 | tf_op jit(solution)/shard_map/all_to_all | solution.py:56
  34.1 20.2 %collective-permute-start.2 = (bf16[128,256]{0,1:T(8,128)(2,1)S(1)}, bf16[128,256]{0,1:T(8,128)(2,1)S(1)}, u32[]{:S(2)}, u32[]{:S(2)}) collective-permute-start(bf16[128,256]{0,1:T(8,128)(2,1)S(1)} %pad_maximum_fusion), channel_id=1, source_target_pairs={{0,8},{8,16},{16,24},{24,32},{32,40},{40,48},{48,56},{56,64},{64,7... | collective-permute-start | bytes 196616 | tf_op jit(solution)/shard_map/ppermute | solution.py:19
  37.6 16.7 %collective-permute-start.1 = (bf16[128,256]{0,1:T(8,128)(2,1)S(1)}, bf16[128,256]{0,1:T(8,128)(2,1)S(1)}, u32[]{:S(2)}, u32[]{:S(2)}) collective-permute-start(bf16[128,256]{0,1:T(8,128)(2,1)S(1)} %pad_maximum_fusion), channel_id=1, source_target_pairs={{0,16},{8,24},{16,32},{24,40},{32,48},{40,56},{48,64},{56,72},{64,... | collective-permute-start | bytes 196616 | tf_op jit(solution)/shard_map/ppermute | solution.py:19
  40.7 13.6 %collective-permute-start = (bf16[128,256]{0,1:T(8,128)(2,1)S(1)}, bf16[128,256]{0,1:T(8,128)(2,1)S(1)}, u32[]{:S(2)}, u32[]{:S(2)}) collective-permute-start(bf16[128,256]{0,1:T(8,128)(2,1)S(1)} %pad_maximum_fusion), channel_id=1, source_target_pairs={{0,24},{8,32},{16,40},{24,48},{32,56},{40,64},{48,72},{56,80},{64,... | collective-permute-start | bytes 196616 | tf_op jit(solution)/shard_map/ppermute | solution.py:19
  45.3 19.1 %all-to-all-start.1 = ((bf16[64,2,256]{2,1,0:T(2,128)(2,1)}), bf16[64,2,256]{2,1,0:T(2,128)(2,1)S(1)}, u32[]{:S(2)}, u32[]{:S(2)}) async-start(bf16[64,2,256]{2,1,0:T(2,128)(2,1)} %all_to_all.10), calls=%async_computation.1 | async-start | bytes 131072 | tf_op jit(solution)/shard_map/all_to_all | solution.py:106

commit v4 on v1

--- a/solution.py
+++ b/solution.py
@@ -5,9 +5,8 @@
 from jax import lax
 from jax.sharding import PartitionSpec as P
 
+
 HD = 128
-HQ = 32
-KVH = 4
 BACK = 3
 
 
@@ -41,7 +40,7 @@
     return (segment, indices - start)
 
 
-def local(tokens, kv_weight, queries, lengths, page_owner):
+def layer(tokens, kv_weight, queries, lengths, page_owner):
     rows = tokens.shape[0]
     tp_size = lax.axis_size("tp")
     tp_index = lax.axis_index("tp")
@@ -50,14 +49,14 @@
     segment, positions = segment_info(lengths, local_index)
     local_heads = queries.shape[1] // HD
     partial_value = jnp.dot(tokens, kv_weight, preferred_element_type=jnp.float32)
-    own = lax.psum_scatter(partial_value, "tp", scatter_dimension=1, tiled=True)
+    pieces = partial_value.astype(jnp.bfloat16).reshape(rows, tp_size, HD)
+    arrived = lax.all_to_all(jnp.transpose(pieces, (1, 0, 2)), "tp", 0, 0, tiled=True)
+    own = jnp.sum(arrived.astype(jnp.float32), axis=0)
     is_key = tp_index % 2 == 0
     turned = rotate(own.reshape(rows, 1, HD), positions).reshape(rows, HD)
     mine = jnp.where(is_key, turned, own).astype(jnp.bfloat16)
     other = lax.ppermute(mine, "tp", [(i, i ^ 1) for i in range(tp_size)])
-    key_now = jnp.where(is_key, mine, other)
-    value_now = jnp.where(is_key, other, mine)
-    near = jnp.concatenate([key_now, value_now], axis=1)
+    near = jnp.concatenate([jnp.where(is_key, mine, other), jnp.where(is_key, other, mine)], axis=1)
     rotated = rotate(queries.astype(jnp.float32).reshape(rows, local_heads, HD), positions).astype(
         jnp.bfloat16
     )
@@ -68,7 +67,7 @@
     window = jnp.concatenate(blocks, axis=0)
     key_total = (BACK + 1) * rows
     key_index = (req_index - BACK) * rows + jnp.arange(key_total, dtype=jnp.int32)
-    key_segment, unused = segment_info(lengths, key_index)
+    key_segment, _ = segment_info(lengths, key_index)
     allowed = (
         (key_index[None, :] >= 0)
         & (key_index[None, :] <= local_index[:, None])
@@ -111,4 +110,4 @@
 def solution(mesh):
     in_specs = (P("req", "tp"), P("tp", None), P("req", "tp"), P(), P("req", None))
     out_specs = (P("req", "tp"), P("req", "tp"))
-    return jax.shard_map(local, mesh=mesh, in_specs=in_specs, out_specs=out_specs, check_vma=False)
+    return jax.shard_map(layer, mesh=mesh, in_specs=in_specs, out_specs=out_specs, check_vma=False)

time: 103 us -> 65 us (0.63)
  waiting for transfers between devices: 49.7 us -> 19.5 us
  between operations: 14.3 us -> 0.91 us
  starting transfers between devices: 28.4 us -> 34.9 us
    reduce_scatter x1 -> x0, waiting for transfers between devices: 40.2 us -> none  [local(): own = lax.psum_scatter(partial_value, 'tp', scatter_dimension=1, tiled=True)]
    all_to_all x1 -> x2, starting transfers between devices: 9.93 us -> 19.9 us  [the longest x1 10.9 us: layer(): lax.all_to_all(jnp.transpose(pieces, (1, 0, 2)), 'tp', 0, 0, tiled=True)]
    all_to_all x1 -> x2, waiting for transfers between devices: 7.99 us -> 16.8 us  [the longest x1 8.79 us: layer(): lax.all_to_all(jnp.transpose(pieces, (1, 0, 2)), 'tp', 0, 0, tiled=True)]
    ppermute x3, starting transfers between devices: 15.3 us -> 13.1 us  [shifted(): lax.ppermute(value, axis, [(source, source + steps) for source in range(f...]
    ppermute x1, starting transfers between devices: 3.13 us -> 1.92 us  [layer(): other = lax.ppermute(mine, 'tp', [(i, i ^ 1) for i in range(tp_size)])]
    ppermute x1, waiting for transfers between devices: 1.48 us -> 2.67 us  [layer(): other = lax.ppermute(mine, 'tp', [(i, i ^ 1) for i in range(tp_size)])]
  transfers between devices with their start and end apart: 6 -> 6, of which waited for: 3 -> 3; matrix products, arithmetic and copies ran while one was open for 4% -> 6% of each run, Pallas kernels for 0% -> 0%
where the time goes in v4:
time: 65 us; the launch traced here: 64.6 us
  starting transfers between devices  34.9 us (54%)
  waiting for transfers between devices  19.5 us (30%)
  local copies, waits for them, and re-layouts  4.96 us (8%)
  matrix products  2.49 us (4%)
  other arithmetic  1.92 us (3%)
  between operations  0.91 us (1%)
    ppermute x3, starting transfers between devices, shifted(): lax.ppermute(value, axis, [(source, source + steps) for source in range(f...  13.1 us
    all_to_all x1, starting transfers between devices, layer(): lax.all_to_all(jnp.transpose(pieces, (1, 0, 2)), 'tp', 0, 0, tiled=True)  10.9 us
    all_to_all x1, starting transfers between devices, layer(): lax.all_to_all(outgoing, 'req', split_axis=0, concat_axis=0, tiled=True)  9.03 us
    all_to_all x1, waiting for transfers between devices, layer(): lax.all_to_all(jnp.transpose(pieces, (1, 0, 2)), 'tp', 0, 0, tiled=True)  8.79 us
    all_to_all x1, waiting for transfers between devices, layer(): lax.all_to_all(outgoing, 'req', split_axis=0, concat_axis=0, tiled=True)  7.99 us
    unnamed x12, local copies, waits for them, and re-layouts  2.73 us
    ppermute x1, waiting for transfers between devices, layer(): other = lax.ppermute(mine, 'tp', [(i, i ^ 1) for i in range(tp_size)])  2.67 us
    ppermute x1, starting transfers between devices, layer(): other = lax.ppermute(mine, 'tp', [(i, i ^ 1) for i in range(tp_size)])  1.92 us
  transfers between devices with their start and end apart: 6, of which 3 were waited for; matrix products, arithmetic and copies ran while one was open for 6% of the time, Pallas kernels for 0%

profile of v4, /device:TPU:1, one launch (start us, length us, event | category | flops | bytes accessed | tf_op | source)
XLA Modules:
  0.0 64.6 jit_solution(12787787243554979483)
XLA Ops:
  0.6 0.0 copy-start
  0.6 0.0 copy-start.3
  0.7 0.0 copy-start.2
  0.7 1.6 %copy-done = bf16[1024,1024]{1,0:T(8,128)(2,1)S(1)} copy-done((bf16[1024,1024]{1,0:T(8,128)(2,1)S(1)}, bf16[1024,1024]{1,0:T(8,128)(2,1)}, u32[]{:S(2)}) %copy-start) | copy-done | bytes 2097176
  2.2 0.0 copy-start.1
  2.2 1.4 %fusion.1 = bf16[16,8,8,128]{3,2,1,0:T(8,128)(2,1)S(1)} fusion(bf16[128,1024]{1,0:T(8,128)(2,1)} %param.5, bf16[1024,1024]{1,0:T(8,128)(2,1)S(1)} %copy-done), kind=kOutput, calls=%fused_computation.3 | convolution fusion | flops 268566528 | bytes 2621440 | tf_op jit(solution)/shard_map/dot_general | solution.py:51
  3.7 0.7 %copy.36 = bf16[16,8,8,128]{3,2,0,1:T(8,128)(2,1)} copy(bf16[16,8,8,128]{3,2,1,0:T(8,128)(2,1)S(1)} %fusion.1) | data formatting | bytes 524288 | tf_op jit(solution)/shard_map/reshape | solution.py:52
  4.4 10.9 %all-to-all-start = ((bf16[8,128,128]{2,1,0:T(8,128)(2,1)}), bf16[8,128,128]{2,1,0:T(8,128)(2,1)S(1)}, u32[]{:S(2)}, u32[]{:S(2)}) async-start(bf16[8,128,128]{2,1,0:T(8,128)(2,1)} %bitcast.42), calls=%async_computation | async-start | bytes 524288 | tf_op jit(solution)/shard_map/all_to_all | solution.py:53
  15.3 0.0 copy-done.3
  15.3 0.2 convert_reduce_fusion.2
  15.5 0.0 copy-done.2
  15.5 0.1 copy.23
  15.6 0.1 reduce-window.8
  15.7 0.1 reduce
  15.8 0.1 fusion.21
  15.9 0.1 convert_reduce_fusion.1
  16.0 0.0 copy-done.1
  16.0 0.1 copy.24
  16.1 0.1 copy.33
  16.3 0.1 copy.32
  16.4 0.3 multiply_cosine_fusion.1
  16.7 0.1 compare_and_fusion
  16.9 0.1 subtract_convert_fusion
  17.0 8.8 %all-to-all-done = bf16[8,128,128]{2,1,0:T(8,128)(2,1)S(1)} async-done(((bf16[8,128,128]{2,1,0:T(8,128)(2,1)}), bf16[8,128,128]{2,1,0:T(8,128)(2,1)S(1)}, u32[]{:S(2)}, u32[]{:S(2)}) %all-to-all-start) | async-done | bytes 262176 | tf_op jit(solution)/shard_map/all_to_all | solution.py:53
  25.8 0.3 fusion.14
  26.1 0.1 fusion.16
  26.2 1.9 %collective-permute-start = (bf16[128,128]{1,0:T(8,128)(2,1)S(1)}, bf16[128,128]{1,0:T(8,128)(2,1)S(1)}, u32[]{:S(2)}, u32[]{:S(2)}) collective-permute-start(bf16[128,128]{1,0:T(8,128)(2,1)S(1)} %get-tuple-element.12), channel_id=1, source_target_pairs={{0,1},{1,0},{2,3},{3,2},{4,5},{5,4},{6,7},{7,6},{8,9},{9,8},{10,11... | collective-permute-start | bytes 98312 | tf_op jit(solution)/shard_map/ppermute | solution.py:58
  28.2 2.7 %collective-permute-done = bf16[128,128]{1,0:T(8,128)(2,1)S(1)} collective-permute-done((bf16[128,128]{1,0:T(8,128)(2,1)S(1)}, bf16[128,128]{1,0:T(8,128)(2,1)S(1)}, u32[]{:S(2)}, u32[]{:S(2)}) %collective-permute-start) | collective-permute-done | bytes 32800 | tf_op jit(solution)/shard_map/ppermute | solution.py:58
  30.9 6.5 %collective-permute-start.3 = (bf16[128,256]{1,0:T(8,128)(2,1)S(1)}, bf16[128,256]{1,0:T(8,128)(2,1)S(1)}, u32[]{:S(2)}, u32[]{:S(2)}) collective-permute-start(bf16[128,256]{1,0:T(8,128)(2,1)S(1)} %pad_maximum_fusion.1), channel_id=1, source_target_pairs={{0,8},{8,16},{16,24},{24,32},{32,40},{40,48},{48,56},{56,64},{64,7... | collective-permute-start | bytes 196616 | tf_op jit(solution)/shard_map/ppermute | solution.py:19
  37.4 3.1 %collective-permute-start.2 = (bf16[128,256]{1,0:T(8,128)(2,1)S(1)}, bf16[128,256]{1,0:T(8,128)(2,1)S(1)}, u32[]{:S(2)}, u32[]{:S(2)}) collective-permute-start(bf16[128,256]{1,0:T(8,128)(2,1)S(1)} %pad_maximum_fusion.1), channel_id=1, source_target_pairs={{0,16},{8,24},{16,32},{24,40},{32,48},{40,56},{48,64},{56,72},{64,... | collective-permute-start | bytes 196616 | tf_op jit(solution)/shard_map/ppermute | solution.py:19
  40.5 3.4 %collective-permute-start.1 = (bf16[128,256]{1,0:T(8,128)(2,1)S(1)}, bf16[128,256]{1,0:T(8,128)(2,1)S(1)}, u32[]{:S(2)}, u32[]{:S(2)}) collective-permute-start(bf16[128,256]{1,0:T(8,128)(2,1)S(1)} %pad_maximum_fusion.1), channel_id=1, source_target_pairs={{0,24},{8,32},{16,40},{24,48},{32,56},{40,64},{48,72},{56,80},{64,... | collective-permute-start | bytes 196616 | tf_op jit(solution)/shard_map/ppermute | solution.py:19
  44.0 0.1 convolution_convert_fusion.1
  44.1 0.7 %all_to_all.10 = bf16[64,2,256]{2,1,0:T(2,128)(2,1)} reshape(bf16[128,256]{1,0:T(8,128)(2,1)S(1)} %convolution_convert_fusion.1) | data formatting | bytes 131072 | tf_op jit(solution)/shard_map/all_to_all | solution.py:105
  44.8 9.0 %all-to-all-start.1 = ((bf16[64,2,256]{2,1,0:T(2,128)(2,1)}), bf16[64,2,256]{2,1,0:T(2,128)(2,1)S(1)}, u32[]{:S(2)}, u32[]{:S(2)}) async-start(bf16[64,2,256]{2,1,0:T(2,128)(2,1)} %all_to_all.10), calls=%async_computation.1 | async-start | bytes 131072 | tf_op jit(solution)/shard_map/all_to_all | solution.py:105
  53.8 0.0 collective-permute-done.3
  53.9 0.0 collective-permute-done.2
  53.9 0.0 collective-permute-done.1
  53.9 0.5 fusion.24
  54.4 0.3 fusion.4
  54.7 0.5 fusion.3
  55.2 0.8 %copy.29 = bf16[128,512]{1,0:T(8,128)(2,1)} copy(bf16[128,512]{0,1:T(8,128)(2,1)S(1)} %bitcast.45) | data formatting | bytes 262144
  55.9 8.0 %all-to-all-done.1 = bf16[64,2,256]{2,1,0:T(2,128)(2,1)S(1)} async-done(((bf16[64,2,256]{2,1,0:T(2,128)(2,1)}), bf16[64,2,256]{2,1,0:T(2,128)(2,1)S(1)}, u32[]{:S(2)}, u32[]{:S(2)}) %all-to-all-start.1) | async-done | bytes 65568 | tf_op jit(solution)/shard_map/all_to_all | solution.py:105
  63.9 0.7 %reshape.270 = bf16[256,128]{1,0:T(8,128)(2,1)} reshape(bf16[64,2,256]{2,1,0:T(2,128)(2,1)S(1)} %all-to-all-done.1) | data formatting | bytes 131072 | tf_op jit(solution)/shard_map/reshape | solution.py:106
  (13 shorter events, 0.2 us)
Async XLA Ops:
  0.6 1.6 %copy-start = (bf16[1024,1024]{1,0:T(8,128)(2,1)S(1)}, bf16[1024,1024]{1,0:T(8,128)(2,1)}, u32[]{:S(2)}) copy-start(bf16[1024,1024]{1,0:T(8,128)(2,1)} %param.6) | copy-start | bytes 6291460
  0.6 14.7 %copy-start.3 = (s32[64,1]{0,1:T(1,128)S(1)}, s32[64,1]{0,1:T(1,128)}, u32[]{:S(2)}) copy-start(s32[64,1]{0,1:T(1,128)} %param.9) | copy-start | bytes 772
  0.7 14.9 %copy-start.2 = (s32[32]{0:T(128)S(1)}, s32[32]{0:T(128)}, u32[]{:S(2)}) copy-start(s32[32]{0:T(128)} %param.8) | copy-start | bytes 388
  2.2 13.8 %copy-start.1 = (bf16[128,512]{1,0:T(8,128)(2,1)S(1)}, bf16[128,512]{1,0:T(8,128)(2,1)}, u32[]{:S(2)}) copy-start(bf16[128,512]{1,0:T(8,128)(2,1)} %param.7) | copy-start | bytes 393220
  4.4 21.3 %all-to-all-start = ((bf16[8,128,128]{2,1,0:T(8,128)(2,1)}), bf16[8,128,128]{2,1,0:T(8,128)(2,1)S(1)}, u32[]{:S(2)}, u32[]{:S(2)}) async-start(bf16[8,128,128]{2,1,0:T(8,128)(2,1)} %bitcast.42), calls=%async_computation | async-start | bytes 524288 | tf_op jit(solution)/shard_map/all_to_all | solution.py:53
  26.2 4.7 %collective-permute-start = (bf16[128,128]{1,0:T(8,128)(2,1)S(1)}, bf16[128,128]{1,0:T(8,128)(2,1)S(1)}, u32[]{:S(2)}, u32[]{:S(2)}) collective-permute-start(bf16[128,128]{1,0:T(8,128)(2,1)S(1)} %get-tuple-element.12), channel_id=1, source_target_pairs={{0,1},{1,0},{2,3},{3,2},{4,5},{5,4},{6,7},{7,6},{8,9},{9,8},{10,11... | collective-permute-start | bytes 98312 | tf_op jit(solution)/shard_map/ppermute | solution.py:58
  30.9 22.9 %collective-permute-start.3 = (bf16[128,256]{1,0:T(8,128)(2,1)S(1)}, bf16[128,256]{1,0:T(8,128)(2,1)S(1)}, u32[]{:S(2)}, u32[]{:S(2)}) collective-permute-start(bf16[128,256]{1,0:T(8,128)(2,1)S(1)} %pad_maximum_fusion.1), channel_id=1, source_target_pairs={{0,8},{8,16},{16,24},{24,32},{32,40},{40,48},{48,56},{56,64},{64,7... | collective-permute-start | bytes 196616 | tf_op jit(solution)/shard_map/ppermute | solution.py:19
  37.4 16.4 %collective-permute-start.2 = (bf16[128,256]{1,0:T(8,128)(2,1)S(1)}, bf16[128,256]{1,0:T(8,128)(2,1)S(1)}, u32[]{:S(2)}, u32[]{:S(2)}) collective-permute-start(bf16[128,256]{1,0:T(8,128)(2,1)S(1)} %pad_maximum_fusion.1), channel_id=1, source_target_pairs={{0,16},{8,24},{16,32},{24,40},{32,48},{40,56},{48,64},{56,72},{64,... | collective-permute-start | bytes 196616 | tf_op jit(solution)/shard_map/ppermute | solution.py:19
  40.5 13.3 %collective-permute-start.1 = (bf16[128,256]{1,0:T(8,128)(2,1)S(1)}, bf16[128,256]{1,0:T(8,128)(2,1)S(1)}, u32[]{:S(2)}, u32[]{:S(2)}) collective-permute-start(bf16[128,256]{1,0:T(8,128)(2,1)S(1)} %pad_maximum_fusion.1), channel_id=1, source_target_pairs={{0,24},{8,32},{16,40},{24,48},{32,56},{40,64},{48,72},{56,80},{64,... | collective-permute-start | bytes 196616 | tf_op jit(solution)/shard_map/ppermute | solution.py:19
  44.8 19.1 %all-to-all-start.1 = ((bf16[64,2,256]{2,1,0:T(2,128)(2,1)}), bf16[64,2,256]{2,1,0:T(2,128)(2,1)S(1)}, u32[]{:S(2)}, u32[]{:S(2)}) async-start(bf16[64,2,256]{2,1,0:T(2,128)(2,1)} %all_to_all.10), calls=%async_computation.1 | async-start | bytes 131072 | tf_op jit(solution)/shard_map/all_to_all | solution.py:105

commit v5 on v4

--- a/solution.py
+++ b/solution.py
@@ -97,12 +97,19 @@
     order = jnp.arange(pages_here, dtype=jnp.int32)
     earlier = (owners[:, None] == owners[None, :]) & (order[None, :] < order[:, None])
     rank = jnp.sum(earlier.astype(jnp.int32), axis=1)
-    target = owners * capacity + rank
-    slots = lax.axis_size("req") * capacity
+    count = lax.axis_size("req")
+    side = math.isqrt(count)
+    assert side * side == count
+    target = (owners % side) * (side * capacity) + (owners // side) * capacity + rank
+    slots = count * capacity
     placing = (jnp.arange(slots, dtype=jnp.int32)[:, None] == target[None, :]).astype(jnp.bfloat16)
     paged = mine.reshape(pages_here, page_rows * share)
     outgoing = jnp.dot(placing, paged, preferred_element_type=jnp.float32).astype(jnp.bfloat16)
-    incoming = lax.all_to_all(outgoing, "req", split_axis=0, concat_axis=0, tiled=True)
+    lows = [[side * a + b for b in range(side)] for a in range(side)]
+    highs = [[side * a + b for a in range(side)] for b in range(side)]
+    middle = lax.all_to_all(outgoing, "req", 0, 0, tiled=True, axis_index_groups=lows)
+    middle = jnp.transpose(middle.reshape(side, side, capacity, -1), (1, 0, 2, 3)).reshape(slots, -1)
+    incoming = lax.all_to_all(middle, "req", 0, 0, tiled=True, axis_index_groups=highs)
     cache = incoming.reshape(slots * page_rows, share)
     return (attended, cache)
 

time: 65 us -> 62.7 us (0.965)
  waiting for transfers between devices: 19.5 us -> 14.3 us
  starting transfers between devices: 34.9 us -> 36.9 us
    all_to_all x1 -> x2, starting transfers between devices: 9.03 us -> 14 us  [the longest x1 7.2 us: layer(): lax.all_to_all(outgoing, 'req', 0, 0, tiled=True, axis_index_groups=lows)]
    ppermute x3, starting transfers between devices: 13.1 us -> 10.1 us  [shifted(): lax.ppermute(value, axis, [(source, source + steps) for source in range(f...]
    ppermute x1, waiting for transfers between devices: 2.67 us -> 0.01 us  [layer(): other = lax.ppermute(mine, 'tp', [(i, i ^ 1) for i in range(tp_size)])]
    all_to_all x1 -> x2, waiting for transfers between devices: 7.99 us -> 5.33 us  [the longest x1 5.33 us: layer(): lax.all_to_all(middle, 'req', 0, 0, tiled=True, axis_index_groups=highs)]
  transfers between devices with their start and end apart: 6 -> 7, of which waited for: 3 -> 2; matrix products, arithmetic and copies ran while one was open for 6% -> 7% of each run, Pallas kernels for 0% -> 0%
where the time goes in v5:
time: 62.7 us; the launch traced here: 62.2 us
  starting transfers between devices  36.9 us (59%)
  waiting for transfers between devices  14.3 us (23%)
  local copies, waits for them, and re-layouts  5.01 us (8%)
  matrix products  3.13 us (5%)
  other arithmetic  1.93 us (3%)
  between operations  0.92 us (1%)
    all_to_all x1, starting transfers between devices, layer(): lax.all_to_all(jnp.transpose(pieces, (1, 0, 2)), 'tp', 0, 0, tiled=True)  10.9 us
    ppermute x3, starting transfers between devices, shifted(): lax.ppermute(value, axis, [(source, source + steps) for source in range(f...  10.1 us
    all_to_all x1, waiting for transfers between devices, layer(): lax.all_to_all(jnp.transpose(pieces, (1, 0, 2)), 'tp', 0, 0, tiled=True)  8.92 us
    all_to_all x1, starting transfers between devices, layer(): lax.all_to_all(outgoing, 'req', 0, 0, tiled=True, axis_index_groups=lows)  7.2 us
    all_to_all x1, starting transfers between devices, layer(): lax.all_to_all(middle, 'req', 0, 0, tiled=True, axis_index_groups=highs)  6.82 us
    all_to_all x1, waiting for transfers between devices, layer(): lax.all_to_all(middle, 'req', 0, 0, tiled=True, axis_index_groups=highs)  5.33 us
    unnamed x12, local copies, waits for them, and re-layouts  2.73 us
    ppermute x1, starting transfers between devices, layer(): other = lax.ppermute(mine, 'tp', [(i, i ^ 1) for i in range(tp_size)])  1.92 us
  transfers between devices with their start and end apart: 7, of which 2 were waited for; matrix products, arithmetic and copies ran while one was open for 7% of the time, Pallas kernels for 0%

profile of v5, /device:TPU:1, one launch (start us, length us, event | category | flops | bytes accessed | tf_op | source)
XLA Modules:
  0.0 62.2 jit_solution(16421313618071520882)
XLA Ops:
  0.6 0.0 copy-start
  0.6 0.0 copy-start.3
  0.7 0.0 copy-start.2
  0.7 1.6 %copy-done = bf16[1024,1024]{1,0:T(8,128)(2,1)S(1)} copy-done((bf16[1024,1024]{1,0:T(8,128)(2,1)S(1)}, bf16[1024,1024]{1,0:T(8,128)(2,1)}, u32[]{:S(2)}) %copy-start) | copy-done | bytes 2097176
  2.2 0.0 copy-start.1
  2.2 1.4 %fusion.1 = bf16[16,8,8,128]{3,2,1,0:T(8,128)(2,1)S(1)} fusion(bf16[128,1024]{1,0:T(8,128)(2,1)} %param.5, bf16[1024,1024]{1,0:T(8,128)(2,1)S(1)} %copy-done), kind=kOutput, calls=%fused_computation.3 | convolution fusion | flops 268566528 | bytes 2621440 | tf_op jit(solution)/shard_map/dot_general | solution.py:51
  3.7 0.7 %copy.40 = bf16[16,8,8,128]{3,2,0,1:T(8,128)(2,1)} copy(bf16[16,8,8,128]{3,2,1,0:T(8,128)(2,1)S(1)} %fusion.1) | data formatting | bytes 524288 | tf_op jit(solution)/shard_map/reshape | solution.py:52
  4.4 10.9 %all-to-all-start = ((bf16[8,128,128]{2,1,0:T(8,128)(2,1)}), bf16[8,128,128]{2,1,0:T(8,128)(2,1)S(1)}, u32[]{:S(2)}, u32[]{:S(2)}) async-start(bf16[8,128,128]{2,1,0:T(8,128)(2,1)} %bitcast.44), calls=%async_computation | async-start | bytes 524288 | tf_op jit(solution)/shard_map/all_to_all | solution.py:53
  15.3 0.0 copy-done.3
  15.3 0.2 convert_reduce_fusion.2
  15.5 0.0 copy-done.2
  15.5 0.1 copy.26
  15.6 0.1 reduce-window.8
  15.7 0.1 reduce
  15.8 0.1 fusion.21
  15.9 0.1 convert_reduce_fusion.1
  16.0 0.0 copy-done.1
  16.0 0.1 copy.27
  16.1 0.1 copy.37
  16.3 0.1 copy.36
  16.4 0.3 multiply_cosine_fusion.1
  16.7 0.1 subtract_convert_fusion
  16.8 8.9 %all-to-all-done = bf16[8,128,128]{2,1,0:T(8,128)(2,1)S(1)} async-done(((bf16[8,128,128]{2,1,0:T(8,128)(2,1)}), bf16[8,128,128]{2,1,0:T(8,128)(2,1)S(1)}, u32[]{:S(2)}, u32[]{:S(2)}) %all-to-all-start) | async-done | bytes 262176 | tf_op jit(solution)/shard_map/all_to_all | solution.py:53
  25.8 0.3 fusion.14
  26.1 0.1 fusion.16
  26.3 1.9 %collective-permute-start = (bf16[128,128]{1,0:T(8,128)(2,1)S(1)}, bf16[128,128]{1,0:T(8,128)(2,1)S(1)}, u32[]{:S(2)}, u32[]{:S(2)}) collective-permute-start(bf16[128,128]{1,0:T(8,128)(2,1)S(1)} %get-tuple-element.12), channel_id=1, source_target_pairs={{0,1},{1,0},{2,3},{3,2},{4,5},{5,4},{6,7},{7,6},{8,9},{9,8},{10,11... | collective-permute-start | bytes 98312 | tf_op jit(solution)/shard_map/ppermute | solution.py:58
  28.2 0.8 %convolution_convert_fusion.1 = bf16[128,256]{1,0:T(8,128)(2,1)} fusion(bf16[64,256]{1,0:T(8,128)(2,1)S(1)} %reshape.323, bf16[64,256]{1,0:T(8,128)(2,1)S(1)} %reduce_sum.62, s32[64]{0:T(128)S(1)} %fusion.24, pred[]{:T(512)S(6)} %eq.53), kind=kOutput, calls=%fused_computation.7 | convolution fusion | flops 4251648 | bytes 131329 | tf_op jit(solution)/shard_map/dot_general | solution.py:107
  29.0 7.2 %all-to-all-start.1 = ((bf16[8,16,256]{2,1,0:T(8,128)(2,1)}), bf16[8,16,256]{2,1,0:T(8,128)(2,1)S(1)}, u32[]{:S(2)}, u32[]{:S(2)}) async-start(bf16[8,16,256]{2,1,0:T(8,128)(2,1)} %bitcast.13), calls=%async_computation.1 | async-start | bytes 131072 | tf_op jit(solution)/shard_map/all_to_all | solution.py:110
  36.2 0.0 collective-permute-done
  36.2 3.5 %collective-permute-start.3 = (bf16[128,256]{1,0:T(8,128)(2,1)S(1)}, bf16[128,256]{1,0:T(8,128)(2,1)S(1)}, u32[]{:S(2)}, u32[]{:S(2)}) collective-permute-start(bf16[128,256]{1,0:T(8,128)(2,1)S(1)} %pad_maximum_fusion.1), channel_id=1, source_target_pairs={{0,8},{8,16},{16,24},{24,32},{32,40},{40,48},{48,56},{56,64},{64,7... | collective-permute-start | bytes 196616 | tf_op jit(solution)/shard_map/ppermute | solution.py:19
  39.7 3.1 %collective-permute-start.2 = (bf16[128,256]{1,0:T(8,128)(2,1)S(1)}, bf16[128,256]{1,0:T(8,128)(2,1)S(1)}, u32[]{:S(2)}, u32[]{:S(2)}) collective-permute-start(bf16[128,256]{1,0:T(8,128)(2,1)S(1)} %pad_maximum_fusion.1), channel_id=1, source_target_pairs={{0,16},{8,24},{16,32},{24,40},{32,48},{40,56},{48,64},{56,72},{64,... | collective-permute-start | bytes 196616 | tf_op jit(solution)/shard_map/ppermute | solution.py:19
  42.8 3.5 %collective-permute-start.1 = (bf16[128,256]{1,0:T(8,128)(2,1)S(1)}, bf16[128,256]{1,0:T(8,128)(2,1)S(1)}, u32[]{:S(2)}, u32[]{:S(2)}) collective-permute-start(bf16[128,256]{1,0:T(8,128)(2,1)S(1)} %pad_maximum_fusion.1), channel_id=1, source_target_pairs={{0,24},{8,32},{16,40},{24,48},{32,56},{40,64},{48,72},{56,80},{64,... | collective-permute-start | bytes 196616 | tf_op jit(solution)/shard_map/ppermute | solution.py:19
  46.4 0.1 compare_and_fusion
  46.5 0.0 all-to-all-done.1
  46.6 0.7 %all_to_all.18 = bf16[8,16,256]{2,1,0:T(8,128)(2,1)} reshape(bf16[8,8,2,256]{3,2,1,0:T(2,128)(2,1)S(1)} %copy.32) | data formatting | bytes 131072 | tf_op jit(solution)/shard_map/all_to_all | solution.py:112
  47.3 6.8 %all-to-all-start.2 = ((bf16[8,16,256]{2,1,0:T(8,128)(2,1)}), bf16[8,16,256]{2,1,0:T(8,128)(2,1)S(1)}, u32[]{:S(2)}, u32[]{:S(2)}) async-start(bf16[8,16,256]{2,1,0:T(8,128)(2,1)} %all_to_all.18), calls=%async_computation.2 | async-start | bytes 131072 | tf_op jit(solution)/shard_map/all_to_all | solution.py:112
  54.1 0.0 collective-permute-done.3
  54.1 0.0 collective-permute-done.2
  54.1 0.0 collective-permute-done.1
  54.2 0.5 fusion.27
  54.6 0.3 fusion.4
  55.0 0.5 fusion.3
  55.4 0.8 %copy.33 = bf16[128,512]{1,0:T(8,128)(2,1)} copy(bf16[128,512]{0,1:T(8,128)(2,1)S(1)} %bitcast.48) | data formatting | bytes 262144
  56.2 5.3 %all-to-all-done.2 = bf16[8,16,256]{2,1,0:T(8,128)(2,1)S(1)} async-done(((bf16[8,16,256]{2,1,0:T(8,128)(2,1)}), bf16[8,16,256]{2,1,0:T(8,128)(2,1)S(1)}, u32[]{:S(2)}, u32[]{:S(2)}) %all-to-all-start.2) | async-done | bytes 65568 | tf_op jit(solution)/shard_map/all_to_all | solution.py:112
  61.5 0.7 %reshape.325 = bf16[256,128]{1,0:T(8,128)(2,1)} reshape(bf16[8,16,256]{2,1,0:T(8,128)(2,1)S(1)} %all-to-all-done.2) | data formatting | bytes 131072 | tf_op jit(solution)/shard_map/reshape | solution.py:113
  (15 shorter events, 0.3 us)
Async XLA Ops:
  0.6 1.6 %copy-start = (bf16[1024,1024]{1,0:T(8,128)(2,1)S(1)}, bf16[1024,1024]{1,0:T(8,128)(2,1)}, u32[]{:S(2)}) copy-start(bf16[1024,1024]{1,0:T(8,128)(2,1)} %param.6) | copy-start | bytes 6291460
  0.6 14.7 %copy-start.3 = (s32[64,1]{0,1:T(1,128)S(1)}, s32[64,1]{0,1:T(1,128)}, u32[]{:S(2)}) copy-start(s32[64,1]{0,1:T(1,128)} %param.9) | copy-start | bytes 772
  0.7 14.9 %copy-start.2 = (s32[32]{0:T(128)S(1)}, s32[32]{0:T(128)}, u32[]{:S(2)}) copy-start(s32[32]{0:T(128)} %param.8) | copy-start | bytes 388
  2.2 13.8 %copy-start.1 = (bf16[128,512]{1,0:T(8,128)(2,1)S(1)}, bf16[128,512]{1,0:T(8,128)(2,1)}, u32[]{:S(2)}) copy-start(bf16[128,512]{1,0:T(8,128)(2,1)} %param.7) | copy-start | bytes 393220
  4.4 21.3 %all-to-all-start = ((bf16[8,128,128]{2,1,0:T(8,128)(2,1)}), bf16[8,128,128]{2,1,0:T(8,128)(2,1)S(1)}, u32[]{:S(2)}, u32[]{:S(2)}) async-start(bf16[8,128,128]{2,1,0:T(8,128)(2,1)} %bitcast.44), calls=%async_computation | async-start | bytes 524288 | tf_op jit(solution)/shard_map/all_to_all | solution.py:53
  26.3 9.9 %collective-permute-start = (bf16[128,128]{1,0:T(8,128)(2,1)S(1)}, bf16[128,128]{1,0:T(8,128)(2,1)S(1)}, u32[]{:S(2)}, u32[]{:S(2)}) collective-permute-start(bf16[128,128]{1,0:T(8,128)(2,1)S(1)} %get-tuple-element.12), channel_id=1, source_target_pairs={{0,1},{1,0},{2,3},{3,2},{4,5},{5,4},{6,7},{7,6},{8,9},{9,8},{10,11... | collective-permute-start | bytes 98312 | tf_op jit(solution)/shard_map/ppermute | solution.py:58
  29.0 17.5 %all-to-all-start.1 = ((bf16[8,16,256]{2,1,0:T(8,128)(2,1)}), bf16[8,16,256]{2,1,0:T(8,128)(2,1)S(1)}, u32[]{:S(2)}, u32[]{:S(2)}) async-start(bf16[8,16,256]{2,1,0:T(8,128)(2,1)} %bitcast.13), calls=%async_computation.1 | async-start | bytes 131072 | tf_op jit(solution)/shard_map/all_to_all | solution.py:110
  36.2 17.9 %collective-permute-start.3 = (bf16[128,256]{1,0:T(8,128)(2,1)S(1)}, bf16[128,256]{1,0:T(8,128)(2,1)S(1)}, u32[]{:S(2)}, u32[]{:S(2)}) collective-permute-start(bf16[128,256]{1,0:T(8,128)(2,1)S(1)} %pad_maximum_fusion.1), channel_id=1, source_target_pairs={{0,8},{8,16},{16,24},{24,32},{32,40},{40,48},{48,56},{56,64},{64,7... | collective-permute-start | bytes 196616 | tf_op jit(solution)/shard_map/ppermute | solution.py:19
  39.7 14.4 %collective-permute-start.2 = (bf16[128,256]{1,0:T(8,128)(2,1)S(1)}, bf16[128,256]{1,0:T(8,128)(2,1)S(1)}, u32[]{:S(2)}, u32[]{:S(2)}) collective-permute-start(bf16[128,256]{1,0:T(8,128)(2,1)S(1)} %pad_maximum_fusion.1), channel_id=1, source_target_pairs={{0,16},{8,24},{16,32},{24,40},{32,48},{40,56},{48,64},{56,72},{64,... | collective-permute-start | bytes 196616 | tf_op jit(solution)/shard_map/ppermute | solution.py:19
  42.8 11.3 %collective-permute-start.1 = (bf16[128,256]{1,0:T(8,128)(2,1)S(1)}, bf16[128,256]{1,0:T(8,128)(2,1)S(1)}, u32[]{:S(2)}, u32[]{:S(2)}) collective-permute-start(bf16[128,256]{1,0:T(8,128)(2,1)S(1)} %pad_maximum_fusion.1), channel_id=1, source_target_pairs={{0,24},{8,32},{16,40},{24,48},{32,56},{40,64},{48,72},{56,80},{64,... | collective-permute-start | bytes 196616 | tf_op jit(solution)/shard_map/ppermute | solution.py:19
  47.3 14.2 %all-to-all-start.2 = ((bf16[8,16,256]{2,1,0:T(8,128)(2,1)}), bf16[8,16,256]{2,1,0:T(8,128)(2,1)S(1)}, u32[]{:S(2)}, u32[]{:S(2)}) async-start(bf16[8,16,256]{2,1,0:T(8,128)(2,1)} %all_to_all.18), calls=%async_computation.2 | async-start | bytes 131072 | tf_op jit(solution)/shard_map/all_to_all | solution.py:112

commit v6 on v4

--- a/solution.py
+++ b/solution.py
@@ -75,11 +75,10 @@
     )
     key_head = window[:, :HD]
     value_head = window[:, HD:]
-    query_heads = jnp.transpose(rotated, (1, 0, 2))
     scores = lax.dot_general(
-        query_heads, key_head, (((2,), (1,)), ((), ())), preferred_element_type=jnp.float32
+        rotated, key_head, (((2,), (1,)), ((), ())), preferred_element_type=jnp.float32
     ) / math.sqrt(HD)
-    scores = jnp.where(allowed[None], scores, -1e30)
+    scores = jnp.where(allowed[:, None, :], scores, -1e30)
     largest = jnp.max(scores, axis=2, keepdims=True)
     weights = jnp.exp(scores - largest)
     total = jnp.sum(weights, axis=2, keepdims=True)
@@ -87,9 +86,7 @@
         weights.astype(jnp.bfloat16), value_head, (((2,), (0,)), ((), ())),
         preferred_element_type=jnp.float32,
     )
-    outputs = (mixed / total).astype(jnp.bfloat16)
-    attended = jnp.transpose(outputs, (1, 0, 2)).reshape(rows, local_heads * HD)
-    share = mine.shape[1]
+    attended = (mixed / total).astype(jnp.bfloat16).reshape(rows, local_heads * HD)
     pages_here = page_owner.shape[0]
     owners = page_owner[:, 0]
     page_rows = rows // pages_here
@@ -99,11 +96,10 @@
     rank = jnp.sum(earlier.astype(jnp.int32), axis=1)
     target = owners * capacity + rank
     slots = lax.axis_size("req") * capacity
-    placing = (jnp.arange(slots, dtype=jnp.int32)[:, None] == target[None, :]).astype(jnp.bfloat16)
-    paged = mine.reshape(pages_here, page_rows * share)
-    outgoing = jnp.dot(placing, paged, preferred_element_type=jnp.float32).astype(jnp.bfloat16)
-    incoming = lax.all_to_all(outgoing, "req", split_axis=0, concat_axis=0, tiled=True)
-    cache = incoming.reshape(slots * page_rows, share)
+    row_target = (target[:, None] * page_rows + jnp.arange(page_rows, dtype=jnp.int32)[None, :]).reshape(rows)
+    placing = (jnp.arange(slots * page_rows, dtype=jnp.int32)[:, None] == row_target[None, :]).astype(jnp.bfloat16)
+    outgoing = jnp.dot(placing, mine, preferred_element_type=jnp.float32).astype(jnp.bfloat16)
+    cache = lax.all_to_all(outgoing, "req", 0, 0, tiled=True)
     return (attended, cache)
 
 

time: 65 us -> 65.3 us (level)
    all_to_all x1, starting transfers between devices: 9.03 us -> 10.3 us  [layer(): cache = lax.all_to_all(outgoing, 'req', 0, 0, tiled=True)]
    ppermute x3, starting transfers between devices: 13.1 us -> 12.2 us  [shifted(): lax.ppermute(value, axis, [(source, source + steps) for source in range(f...]
    reshape x2 -> x0, local copies, waits for them, and re-layouts: 0.69 us -> none  [the longest x1 0.68 us: layer(): cache = incoming.reshape(slots * page_rows, share)]
    all_to_all x1 -> x0, local copies, waits for them, and re-layouts: 0.67 us -> none  [layer(): lax.all_to_all(outgoing, 'req', split_axis=0, concat_axis=0, tiled=True)]
    unnamed x12 -> x13, local copies, waits for them, and re-layouts: 2.73 us -> 3.36 us
  transfers between devices with their start and end apart: 6 -> 6, of which waited for: 3 -> 3; matrix products, arithmetic and copies ran while one was open for 6% -> 7% of each run, Pallas kernels for 0% -> 0%
where the time goes in v6:
time: 65.3 us; the launch traced here: 64.9 us
  starting transfers between devices  35.3 us (54%)
  waiting for transfers between devices  19.3 us (30%)
  local copies, waits for them, and re-layouts  4.35 us (7%)
  matrix products  3.11 us (5%)
  other arithmetic  2 us (3%)
  between operations  0.9 us (1%)
    ppermute x3, starting transfers between devices, shifted(): lax.ppermute(value, axis, [(source, source + steps) for source in range(f...  12.2 us
    all_to_all x1, starting transfers between devices, layer(): lax.all_to_all(jnp.transpose(pieces, (1, 0, 2)), 'tp', 0, 0, tiled=True)  10.9 us
    all_to_all x1, starting transfers between devices, layer(): cache = lax.all_to_all(outgoing, 'req', 0, 0, tiled=True)  10.3 us
    all_to_all x1, waiting for transfers between devices, layer(): lax.all_to_all(jnp.transpose(pieces, (1, 0, 2)), 'tp', 0, 0, tiled=True)  8.8 us
    all_to_all x1, waiting for transfers between devices, layer(): cache = lax.all_to_all(outgoing, 'req', 0, 0, tiled=True)  7.99 us
    unnamed x13, local copies, waits for them, and re-layouts  3.36 us
    ppermute x1, waiting for transfers between devices, layer(): other = lax.ppermute(mine, 'tp', [(i, i ^ 1) for i in range(tp_size)])  2.51 us
    ppermute x1, starting transfers between devices, layer(): other = lax.ppermute(mine, 'tp', [(i, i ^ 1) for i in range(tp_size)])  1.92 us
  transfers between devices with their start and end apart: 6, of which 3 were waited for; matrix products, arithmetic and copies ran while one was open for 7% of the time, Pallas kernels for 0%

profile of v6, /device:TPU:1, one launch (start us, length us, event | category | flops | bytes accessed | tf_op | source)
XLA Modules:
  0.0 64.9 jit_solution(18218920312770939985)
XLA Ops:
  0.6 0.0 copy-start
  0.6 0.0 copy-start.2
  0.7 0.0 copy-start.1
  0.7 1.6 %copy-done = bf16[1024,1024]{1,0:T(8,128)(2,1)S(1)} copy-done((bf16[1024,1024]{1,0:T(8,128)(2,1)S(1)}, bf16[1024,1024]{1,0:T(8,128)(2,1)}, u32[]{:S(2)}) %copy-start) | copy-done | bytes 2097176
  2.2 0.0 copy-start.3
  2.2 1.4 %fusion.1 = bf16[16,8,8,128]{3,2,1,0:T(8,128)(2,1)S(1)} fusion(bf16[128,1024]{1,0:T(8,128)(2,1)} %param.5, bf16[1024,1024]{1,0:T(8,128)(2,1)S(1)} %copy-done), kind=kOutput, calls=%fused_computation.3 | convolution fusion | flops 268566528 | bytes 2621440 | tf_op jit(solution)/shard_map/dot_general | solution.py:51
  3.6 0.7 %copy.36 = bf16[16,8,8,128]{3,2,0,1:T(8,128)(2,1)} copy(bf16[16,8,8,128]{3,2,1,0:T(8,128)(2,1)S(1)} %fusion.1) | data formatting | bytes 524288 | tf_op jit(solution)/shard_map/reshape | solution.py:52
  4.4 10.9 %all-to-all-start = ((bf16[8,128,128]{2,1,0:T(8,128)(2,1)}), bf16[8,128,128]{2,1,0:T(8,128)(2,1)S(1)}, u32[]{:S(2)}, u32[]{:S(2)}) async-start(bf16[8,128,128]{2,1,0:T(8,128)(2,1)} %bitcast.40), calls=%async_computation | async-start | bytes 524288 | tf_op jit(solution)/shard_map/all_to_all | solution.py:53
  15.3 0.0 copy-done.2
  15.3 0.1 copy.23
  15.4 0.1 reduce-window.8
  15.5 0.1 reduce
  15.6 0.1 fusion.21
  15.7 0.0 copy-done.1
  15.7 0.1 copy.24
  15.9 0.1 copy.32
  16.0 0.1 copy.33
  16.1 0.1 convert_reduce_fusion.1
  16.2 0.0 copy-done.3
  16.2 0.2 convert_reduce_fusion.2
  16.4 0.3 multiply_cosine_fusion.1
  16.7 0.1 compare_and_fusion
  16.9 0.1 subtract_convert_fusion
  17.0 8.8 %all-to-all-done = bf16[8,128,128]{2,1,0:T(8,128)(2,1)S(1)} async-done(((bf16[8,128,128]{2,1,0:T(8,128)(2,1)}), bf16[8,128,128]{2,1,0:T(8,128)(2,1)S(1)}, u32[]{:S(2)}, u32[]{:S(2)}) %all-to-all-start) | async-done | bytes 262176 | tf_op jit(solution)/shard_map/all_to_all | solution.py:53
  25.8 0.3 fusion.14
  26.1 0.1 fusion.17
  26.2 1.9 %collective-permute-start = (bf16[128,128]{1,0:T(8,128)(2,1)S(1)}, bf16[128,128]{1,0:T(8,128)(2,1)S(1)}, u32[]{:S(2)}, u32[]{:S(2)}) collective-permute-start(bf16[128,128]{1,0:T(8,128)(2,1)S(1)} %fusion.17), channel_id=1, source_target_pairs={{0,1},{1,0},{2,3},{3,2},{4,5},{5,4},{6,7},{7,6},{8,9},{9,8},{10,11... | collective-permute-start | bytes 98312 | tf_op jit(solution)/shard_map/ppermute | solution.py:58
  28.1 0.1 iota_add_fusion
  28.2 0.1 add.79
  28.4 2.5 %collective-permute-done = bf16[128,128]{1,0:T(8,128)(2,1)S(1)} collective-permute-done((bf16[128,128]{1,0:T(8,128)(2,1)S(1)}, bf16[128,128]{1,0:T(8,128)(2,1)S(1)}, u32[]{:S(2)}, u32[]{:S(2)}) %collective-permute-start) | collective-permute-done | bytes 32800 | tf_op jit(solution)/shard_map/ppermute | solution.py:58
  30.9 8.0 %collective-permute-start.1 = (bf16[128,256]{1,0:T(8,128)(2,1)S(1)}, bf16[128,256]{1,0:T(8,128)(2,1)S(1)}, u32[]{:S(2)}, u32[]{:S(2)}) collective-permute-start(bf16[128,256]{1,0:T(8,128)(2,1)S(1)} %pad_maximum_fusion), channel_id=1, source_target_pairs={{0,24},{8,32},{16,40},{24,48},{32,56},{40,64},{48,72},{56,80},{64,... | collective-permute-start | bytes 196616 | tf_op jit(solution)/shard_map/ppermute | solution.py:19
  38.9 2.2 %collective-permute-start.2 = (bf16[128,256]{1,0:T(8,128)(2,1)S(1)}, bf16[128,256]{1,0:T(8,128)(2,1)S(1)}, u32[]{:S(2)}, u32[]{:S(2)}) collective-permute-start(bf16[128,256]{1,0:T(8,128)(2,1)S(1)} %pad_maximum_fusion), channel_id=1, source_target_pairs={{0,16},{8,24},{16,32},{24,40},{32,48},{40,56},{48,64},{56,72},{64,... | collective-permute-start | bytes 196616 | tf_op jit(solution)/shard_map/ppermute | solution.py:19
  41.1 1.9 %collective-permute-start.3 = (bf16[128,256]{1,0:T(8,128)(2,1)S(1)}, bf16[128,256]{1,0:T(8,128)(2,1)S(1)}, u32[]{:S(2)}, u32[]{:S(2)}) collective-permute-start(bf16[128,256]{1,0:T(8,128)(2,1)S(1)} %pad_maximum_fusion), channel_id=1, source_target_pairs={{0,8},{8,16},{16,24},{24,32},{32,40},{40,48},{48,56},{56,64},{64,7... | collective-permute-start | bytes 196616 | tf_op jit(solution)/shard_map/ppermute | solution.py:19
  43.1 0.8 %convolution_convert_fusion.1 = bf16[256,128]{1,0:T(8,128)(2,1)} fusion(bf16[128,128]{1,0:T(8,128)(2,1)S(1)} %fusion.17, s32[128]{0:T(128)S(1)} %add.79), kind=kOutput, calls=%fused_computation.6 | convolution fusion | flops 8454144 | bytes 98816 | tf_op jit(solution)/shard_map/dot_general | solution.py:101
  43.9 10.3 %all-to-all-start.1 = ((bf16[64,4,128]{2,1,0:T(4,128)(2,1)}), bf16[64,4,128]{2,1,0:T(4,128)(2,1)S(1)}, u32[]{:S(2)}, u32[]{:S(2)}) async-start(bf16[64,4,128]{2,1,0:T(4,128)(2,1)} %bitcast.12), calls=%async_computation.1 | async-start | bytes 131072 | tf_op jit(solution)/shard_map/all_to_all | solution.py:102
  54.2 0.0 collective-permute-done.1
  54.2 0.0 collective-permute-done.2
  54.2 0.0 collective-permute-done.3
  54.3 0.5 fusion.26
  54.7 0.3 fusion.3
  55.1 0.5 fusion.2
  55.5 0.8 %copy.29 = bf16[128,512]{1,0:T(8,128)(2,1)} copy(bf16[128,512]{0,1:T(8,128)(2,1)S(1)} %bitcast.44) | data formatting | bytes 262144
  56.3 8.0 %all-to-all-done.1 = bf16[64,4,128]{2,1,0:T(4,128)(2,1)S(1)} async-done(((bf16[64,4,128]{2,1,0:T(4,128)(2,1)}), bf16[64,4,128]{2,1,0:T(4,128)(2,1)S(1)}, u32[]{:S(2)}, u32[]{:S(2)}) %all-to-all-start.1) | async-done | bytes 65568 | tf_op jit(solution)/shard_map/all_to_all | solution.py:102
  64.3 0.6 copy.38
  (11 shorter events, 0.1 us)
Async XLA Ops:
  0.6 1.6 %copy-start = (bf16[1024,1024]{1,0:T(8,128)(2,1)S(1)}, bf16[1024,1024]{1,0:T(8,128)(2,1)}, u32[]{:S(2)}) copy-start(bf16[1024,1024]{1,0:T(8,128)(2,1)} %param.6) | copy-start | bytes 6291460
  0.6 14.7 %copy-start.2 = (s32[32]{0:T(128)S(1)}, s32[32]{0:T(128)}, u32[]{:S(2)}) copy-start(s32[32]{0:T(128)} %param.8) | copy-start | bytes 388
  0.7 15.0 %copy-start.1 = (bf16[128,512]{1,0:T(8,128)(2,1)S(1)}, bf16[128,512]{1,0:T(8,128)(2,1)}, u32[]{:S(2)}) copy-start(bf16[128,512]{1,0:T(8,128)(2,1)} %param.7) | copy-start | bytes 393220
  2.2 14.0 %copy-start.3 = (s32[64,1]{0,1:T(1,128)S(1)}, s32[64,1]{0,1:T(1,128)}, u32[]{:S(2)}) copy-start(s32[64,1]{0,1:T(1,128)} %param.9) | copy-start | bytes 772
  4.4 21.4 %all-to-all-start = ((bf16[8,128,128]{2,1,0:T(8,128)(2,1)}), bf16[8,128,128]{2,1,0:T(8,128)(2,1)S(1)}, u32[]{:S(2)}, u32[]{:S(2)}) async-start(bf16[8,128,128]{2,1,0:T(8,128)(2,1)} %bitcast.40), calls=%async_computation | async-start | bytes 524288 | tf_op jit(solution)/shard_map/all_to_all | solution.py:53
  26.2 4.7 %collective-permute-start = (bf16[128,128]{1,0:T(8,128)(2,1)S(1)}, bf16[128,128]{1,0:T(8,128)(2,1)S(1)}, u32[]{:S(2)}, u32[]{:S(2)}) collective-permute-start(bf16[128,128]{1,0:T(8,128)(2,1)S(1)} %fusion.17), channel_id=1, source_target_pairs={{0,1},{1,0},{2,3},{3,2},{4,5},{5,4},{6,7},{7,6},{8,9},{9,8},{10,11... | collective-permute-start | bytes 98312 | tf_op jit(solution)/shard_map/ppermute | solution.py:58
  30.9 23.3 %collective-permute-start.1 = (bf16[128,256]{1,0:T(8,128)(2,1)S(1)}, bf16[128,256]{1,0:T(8,128)(2,1)S(1)}, u32[]{:S(2)}, u32[]{:S(2)}) collective-permute-start(bf16[128,256]{1,0:T(8,128)(2,1)S(1)} %pad_maximum_fusion), channel_id=1, source_target_pairs={{0,24},{8,32},{16,40},{24,48},{32,56},{40,64},{48,72},{56,80},{64,... | collective-permute-start | bytes 196616 | tf_op jit(solution)/shard_map/ppermute | solution.py:19
  38.9 15.3 %collective-permute-start.2 = (bf16[128,256]{1,0:T(8,128)(2,1)S(1)}, bf16[128,256]{1,0:T(8,128)(2,1)S(1)}, u32[]{:S(2)}, u32[]{:S(2)}) collective-permute-start(bf16[128,256]{1,0:T(8,128)(2,1)S(1)} %pad_maximum_fusion), channel_id=1, source_target_pairs={{0,16},{8,24},{16,32},{24,40},{32,48},{40,56},{48,64},{56,72},{64,... | collective-permute-start | bytes 196616 | tf_op jit(solution)/shard_map/ppermute | solution.py:19
  41.1 13.1 %collective-permute-start.3 = (bf16[128,256]{1,0:T(8,128)(2,1)S(1)}, bf16[128,256]{1,0:T(8,128)(2,1)S(1)}, u32[]{:S(2)}, u32[]{:S(2)}) collective-permute-start(bf16[128,256]{1,0:T(8,128)(2,1)S(1)} %pad_maximum_fusion), channel_id=1, source_target_pairs={{0,8},{8,16},{16,24},{24,32},{32,40},{40,48},{48,56},{56,64},{64,7... | collective-permute-start | bytes 196616 | tf_op jit(solution)/shard_map/ppermute | solution.py:19
  43.9 20.4 %all-to-all-start.1 = ((bf16[64,4,128]{2,1,0:T(4,128)(2,1)}), bf16[64,4,128]{2,1,0:T(4,128)(2,1)S(1)}, u32[]{:S(2)}, u32[]{:S(2)}) async-start(bf16[64,4,128]{2,1,0:T(4,128)(2,1)} %bitcast.12), calls=%async_computation.1 | async-start | bytes 131072 | tf_op jit(solution)/shard_map/all_to_all | solution.py:102

commit v7 on v6

--- a/solution.py
+++ b/solution.py
@@ -3,6 +3,7 @@
 import jax
 import jax.numpy as jnp
 from jax import lax
+from jax.experimental import pallas as pl
 from jax.sharding import PartitionSpec as P
 
 
@@ -32,6 +33,27 @@
     )
 
 
+def project_kernel(tokens_ref, weight_ref, out_ref):
+    product = jnp.dot(tokens_ref[...], weight_ref[...], preferred_element_type=jnp.float32)
+    for block in range(out_ref.shape[0]):
+        out_ref[block] = product[:, block * HD : (block + 1) * HD].astype(out_ref.dtype)
+
+
+def project(tokens, kv_weight, per_step=2):
+    rows, features = tokens.shape
+    blocks = kv_weight.shape[1] // HD
+    return pl.pallas_call(
+        project_kernel,
+        grid=(blocks // per_step,),
+        in_specs=[
+            pl.BlockSpec((rows, features), lambda j: (0, 0)),
+            pl.BlockSpec((features, per_step * HD), lambda j: (0, j)),
+        ],
+        out_specs=pl.BlockSpec((per_step, rows, HD), lambda j: (j, 0, 0)),
+        out_shape=jax.ShapeDtypeStruct((blocks, rows, HD), jnp.bfloat16),
+    )(tokens, kv_weight)
+
+
 def segment_info(lengths, indices):
     ends = jnp.cumsum(lengths)
     before = ends[None, :] <= indices[:, None]
@@ -48,9 +70,8 @@
     local_index = req_index * rows + jnp.arange(rows, dtype=jnp.int32)
     segment, positions = segment_info(lengths, local_index)
     local_heads = queries.shape[1] // HD
-    partial_value = jnp.dot(tokens, kv_weight, preferred_element_type=jnp.float32)
-    pieces = partial_value.astype(jnp.bfloat16).reshape(rows, tp_size, HD)
-    arrived = lax.all_to_all(jnp.transpose(pieces, (1, 0, 2)), "tp", 0, 0, tiled=True)
+    pieces = project(tokens, kv_weight)
+    arrived = lax.all_to_all(pieces, "tp", 0, 0, tiled=True)
     own = jnp.sum(arrived.astype(jnp.float32), axis=0)
     is_key = tp_index % 2 == 0
     turned = rotate(own.reshape(rows, 1, HD), positions).reshape(rows, HD)

time: 65.3 us -> 65.6 us (level)
  Pallas kernels: 0 us -> 3.97 us
  local copies, waits for them, and re-layouts: 4.35 us -> 2.04 us
  matrix products: 3.11 us -> 1.7 us
    pallas_call x0 -> x1, Pallas kernels: none -> 3.97 us  [project(): pl.pallas_call(project_kernel, grid=(blocks // per_step,), in_specs=[pl.B...]
    unnamed x13 -> x11, local copies, waits for them, and re-layouts: 3.36 us -> 1.79 us
    dot_general x1 -> x0, matrix products: 1.41 us -> none  [layer(): jnp.dot(tokens, kv_weight, preferred_element_type=jnp.float32)]
    reshape x1 -> x0, local copies, waits for them, and re-layouts: 0.74 us -> none  [layer(): pieces = partial_value.astype(jnp.bfloat16).reshape(rows, tp_size, HD)]
where the time goes in v7:
time: 65.6 us; the launch traced here: 65.2 us
  starting transfers between devices  35.3 us (54%)
  waiting for transfers between devices  19.3 us (29%)
  Pallas kernels  3.97 us (6%)
  local copies, waits for them, and re-layouts  2.04 us (3%)
  other arithmetic  2 us (3%)
  matrix products  1.7 us (3%)
  between operations  0.89 us (1%)
    ppermute x3, starting transfers between devices, shifted(): lax.ppermute(value, axis, [(source, source + steps) for source in range(f...  12.2 us
    all_to_all x1, starting transfers between devices, layer(): arrived = lax.all_to_all(pieces, 'tp', 0, 0, tiled=True)  10.9 us
    all_to_all x1, starting transfers between devices, layer(): cache = lax.all_to_all(outgoing, 'req', 0, 0, tiled=True)  10.4 us
    all_to_all x1, waiting for transfers between devices, layer(): arrived = lax.all_to_all(pieces, 'tp', 0, 0, tiled=True)  8.78 us
    all_to_all x1, waiting for transfers between devices, layer(): cache = lax.all_to_all(outgoing, 'req', 0, 0, tiled=True)  7.99 us
    pallas_call x1, Pallas kernels, project(): pl.pallas_call(project_kernel, grid=(blocks // per_step,), in_specs=[pl.B...  3.97 us
    ppermute x1, waiting for transfers between devices, layer(): other = lax.ppermute(mine, 'tp', [(i, i ^ 1) for i in range(tp_size)])  2.51 us
    ppermute x1, starting transfers between devices, layer(): other = lax.ppermute(mine, 'tp', [(i, i ^ 1) for i in range(tp_size)])  1.92 us
  transfers between devices with their start and end apart: 6, of which 3 were waited for; matrix products, arithmetic and copies ran while one was open for 7% of the time, Pallas kernels for 0%

profile of v7, /device:TPU:1, one launch (start us, length us, event | category | flops | bytes accessed | tf_op | source)
XLA Modules:
  0.0 65.2 jit_solution(9210053689956844708)
XLA Ops:
  0.6 0.0 copy-start.1
  0.6 0.0 copy-start
  0.7 0.0 copy-start.2
  0.7 4.0 %shard_map.68 = bf16[8,128,128]{2,1,0:T(8,128)(2,1)} custom-call(bf16[128,1024]{1,0:T(8,128)(2,1)} %tokens_ref.1, bf16[1024,1024]{1,0:T(8,128)(2,1)} %weight_ref.1), custom_call_target="tpu_custom_call" | custom-call | tf_op jit(solution)/shard_map/pallas_call | solution.py:45
  4.6 10.9 %all-to-all-start = ((bf16[8,128,128]{2,1,0:T(8,128)(2,1)}), bf16[8,128,128]{2,1,0:T(8,128)(2,1)S(1)}, u32[]{:S(2)}, u32[]{:S(2)}) async-start(bf16[8,128,128]{2,1,0:T(8,128)(2,1)} %shard_map.68), calls=%async_computation | async-start | bytes 524288 | tf_op jit(solution)/shard_map/all_to_all | solution.py:74
  15.6 0.0 copy-done.1
  15.6 0.1 copy.16
  15.7 0.1 reduce-window.8
  15.7 0.1 reduce
  15.8 0.1 fusion.20
  15.9 0.0 copy-done
  15.9 0.1 copy.17
  16.1 0.1 copy.24
  16.2 0.1 copy.25
  16.4 0.1 convert_reduce_fusion.1
  16.5 0.0 copy-done.2
  16.5 0.2 convert_reduce_fusion.2
  16.6 0.3 multiply_cosine_fusion.1
  17.0 0.1 compare_and_fusion
  17.1 0.1 subtract_convert_fusion
  17.2 8.8 %all-to-all-done = bf16[8,128,128]{2,1,0:T(8,128)(2,1)S(1)} async-done(((bf16[8,128,128]{2,1,0:T(8,128)(2,1)}), bf16[8,128,128]{2,1,0:T(8,128)(2,1)S(1)}, u32[]{:S(2)}, u32[]{:S(2)}) %all-to-all-start) | async-done | bytes 262176 | tf_op jit(solution)/shard_map/all_to_all | solution.py:74
  26.0 0.3 fusion.13
  26.3 0.1 fusion.16
  26.4 1.9 %collective-permute-start = (bf16[128,128]{1,0:T(8,128)(2,1)S(1)}, bf16[128,128]{1,0:T(8,128)(2,1)S(1)}, u32[]{:S(2)}, u32[]{:S(2)}) collective-permute-start(bf16[128,128]{1,0:T(8,128)(2,1)S(1)} %fusion.16), channel_id=1, source_target_pairs={{0,1},{1,0},{2,3},{3,2},{4,5},{5,4},{6,7},{7,6},{8,9},{9,8},{10,11... | collective-permute-start | bytes 98312 | tf_op jit(solution)/shard_map/ppermute | solution.py:79
  28.4 0.1 iota_add_fusion
  28.4 0.1 add.79
  28.6 2.5 %collective-permute-done = bf16[128,128]{1,0:T(8,128)(2,1)S(1)} collective-permute-done((bf16[128,128]{1,0:T(8,128)(2,1)S(1)}, bf16[128,128]{1,0:T(8,128)(2,1)S(1)}, u32[]{:S(2)}, u32[]{:S(2)}) %collective-permute-start) | collective-permute-done | bytes 32800 | tf_op jit(solution)/shard_map/ppermute | solution.py:79
  31.1 8.0 %collective-permute-start.1 = (bf16[128,256]{1,0:T(8,128)(2,1)S(1)}, bf16[128,256]{1,0:T(8,128)(2,1)S(1)}, u32[]{:S(2)}, u32[]{:S(2)}) collective-permute-start(bf16[128,256]{1,0:T(8,128)(2,1)S(1)} %pad_maximum_fusion), channel_id=1, source_target_pairs={{0,24},{8,32},{16,40},{24,48},{32,56},{40,64},{48,72},{56,80},{64,... | collective-permute-start | bytes 196616 | tf_op jit(solution)/shard_map/ppermute | solution.py:20
  39.2 2.2 %collective-permute-start.2 = (bf16[128,256]{1,0:T(8,128)(2,1)S(1)}, bf16[128,256]{1,0:T(8,128)(2,1)S(1)}, u32[]{:S(2)}, u32[]{:S(2)}) collective-permute-start(bf16[128,256]{1,0:T(8,128)(2,1)S(1)} %pad_maximum_fusion), channel_id=1, source_target_pairs={{0,16},{8,24},{16,32},{24,40},{32,48},{40,56},{48,64},{56,72},{64,... | collective-permute-start | bytes 196616 | tf_op jit(solution)/shard_map/ppermute | solution.py:20
  41.4 1.9 %collective-permute-start.3 = (bf16[128,256]{1,0:T(8,128)(2,1)S(1)}, bf16[128,256]{1,0:T(8,128)(2,1)S(1)}, u32[]{:S(2)}, u32[]{:S(2)}) collective-permute-start(bf16[128,256]{1,0:T(8,128)(2,1)S(1)} %pad_maximum_fusion), channel_id=1, source_target_pairs={{0,8},{8,16},{16,24},{24,32},{32,40},{40,48},{48,56},{56,64},{64,7... | collective-permute-start | bytes 196616 | tf_op jit(solution)/shard_map/ppermute | solution.py:20
  43.3 0.8 %convolution_convert_fusion = bf16[256,128]{1,0:T(8,128)(2,1)} fusion(bf16[128,128]{1,0:T(8,128)(2,1)S(1)} %fusion.16, s32[128]{0:T(128)S(1)} %add.79), kind=kOutput, calls=%fused_computation.4 | convolution fusion | flops 8454144 | bytes 98816 | tf_op jit(solution)/shard_map/dot_general | solution.py:122
  44.1 10.4 %all-to-all-start.1 = ((bf16[64,4,128]{2,1,0:T(4,128)(2,1)}), bf16[64,4,128]{2,1,0:T(4,128)(2,1)S(1)}, u32[]{:S(2)}, u32[]{:S(2)}) async-start(bf16[64,4,128]{2,1,0:T(4,128)(2,1)} %bitcast.11), calls=%async_computation.1 | async-start | bytes 131072 | tf_op jit(solution)/shard_map/all_to_all | solution.py:123
  54.5 0.0 collective-permute-done.1
  54.5 0.0 collective-permute-done.2
  54.5 0.0 collective-permute-done.3
  54.5 0.5 fusion.25
  55.0 0.3 fusion.2
  55.3 0.5 fusion.1
  55.8 0.8 %copy.21 = bf16[128,512]{1,0:T(8,128)(2,1)} copy(bf16[128,512]{0,1:T(8,128)(2,1)S(1)} %bitcast.34) | data formatting | bytes 262144
  56.6 8.0 %all-to-all-done.1 = bf16[64,4,128]{2,1,0:T(4,128)(2,1)S(1)} async-done(((bf16[64,4,128]{2,1,0:T(4,128)(2,1)}), bf16[64,4,128]{2,1,0:T(4,128)(2,1)S(1)}, u32[]{:S(2)}, u32[]{:S(2)}) %all-to-all-start.1) | async-done | bytes 65568 | tf_op jit(solution)/shard_map/all_to_all | solution.py:123
  64.5 0.6 copy.27
  (11 shorter events, 0.1 us)
Async XLA Ops:
  0.6 14.9 %copy-start.1 = (s32[32]{0:T(128)S(1)}, s32[32]{0:T(128)}, u32[]{:S(2)}) copy-start(s32[32]{0:T(128)} %param.8) | copy-start | bytes 388
  0.6 15.3 %copy-start = (bf16[128,512]{1,0:T(8,128)(2,1)S(1)}, bf16[128,512]{1,0:T(8,128)(2,1)}, u32[]{:S(2)}) copy-start(bf16[128,512]{1,0:T(8,128)(2,1)} %param.7) | copy-start | bytes 393220
  0.7 15.8 %copy-start.2 = (s32[64,1]{0,1:T(1,128)S(1)}, s32[64,1]{0,1:T(1,128)}, u32[]{:S(2)}) copy-start(s32[64,1]{0,1:T(1,128)} %param.9) | copy-start | bytes 772
  4.6 21.4 %all-to-all-start = ((bf16[8,128,128]{2,1,0:T(8,128)(2,1)}), bf16[8,128,128]{2,1,0:T(8,128)(2,1)S(1)}, u32[]{:S(2)}, u32[]{:S(2)}) async-start(bf16[8,128,128]{2,1,0:T(8,128)(2,1)} %shard_map.68), calls=%async_computation | async-start | bytes 524288 | tf_op jit(solution)/shard_map/all_to_all | solution.py:74
  26.4 4.7 %collective-permute-start = (bf16[128,128]{1,0:T(8,128)(2,1)S(1)}, bf16[128,128]{1,0:T(8,128)(2,1)S(1)}, u32[]{:S(2)}, u32[]{:S(2)}) collective-permute-start(bf16[128,128]{1,0:T(8,128)(2,1)S(1)} %fusion.16), channel_id=1, source_target_pairs={{0,1},{1,0},{2,3},{3,2},{4,5},{5,4},{6,7},{7,6},{8,9},{9,8},{10,11... | collective-permute-start | bytes 98312 | tf_op jit(solution)/shard_map/ppermute | solution.py:79
  31.1 23.3 %collective-permute-start.1 = (bf16[128,256]{1,0:T(8,128)(2,1)S(1)}, bf16[128,256]{1,0:T(8,128)(2,1)S(1)}, u32[]{:S(2)}, u32[]{:S(2)}) collective-permute-start(bf16[128,256]{1,0:T(8,128)(2,1)S(1)} %pad_maximum_fusion), channel_id=1, source_target_pairs={{0,24},{8,32},{16,40},{24,48},{32,56},{40,64},{48,72},{56,80},{64,... | collective-permute-start | bytes 196616 | tf_op jit(solution)/shard_map/ppermute | solution.py:20
  39.2 15.3 %collective-permute-start.2 = (bf16[128,256]{1,0:T(8,128)(2,1)S(1)}, bf16[128,256]{1,0:T(8,128)(2,1)S(1)}, u32[]{:S(2)}, u32[]{:S(2)}) collective-permute-start(bf16[128,256]{1,0:T(8,128)(2,1)S(1)} %pad_maximum_fusion), channel_id=1, source_target_pairs={{0,16},{8,24},{16,32},{24,40},{32,48},{40,56},{48,64},{56,72},{64,... | collective-permute-start | bytes 196616 | tf_op jit(solution)/shard_map/ppermute | solution.py:20
  41.4 13.1 %collective-permute-start.3 = (bf16[128,256]{1,0:T(8,128)(2,1)S(1)}, bf16[128,256]{1,0:T(8,128)(2,1)S(1)}, u32[]{:S(2)}, u32[]{:S(2)}) collective-permute-start(bf16[128,256]{1,0:T(8,128)(2,1)S(1)} %pad_maximum_fusion), channel_id=1, source_target_pairs={{0,8},{8,16},{16,24},{24,32},{32,40},{40,48},{48,56},{56,64},{64,7... | collective-permute-start | bytes 196616 | tf_op jit(solution)/shard_map/ppermute | solution.py:20
  44.1 20.4 %all-to-all-start.1 = ((bf16[64,4,128]{2,1,0:T(4,128)(2,1)}), bf16[64,4,128]{2,1,0:T(4,128)(2,1)S(1)}, u32[]{:S(2)}, u32[]{:S(2)}) async-start(bf16[64,4,128]{2,1,0:T(4,128)(2,1)} %bitcast.11), calls=%async_computation.1 | async-start | bytes 131072 | tf_op jit(solution)/shard_map/all_to_all | solution.py:123

commit v8 on v6

--- a/solution.py
+++ b/solution.py
@@ -48,10 +48,12 @@
     local_index = req_index * rows + jnp.arange(rows, dtype=jnp.int32)
     segment, positions = segment_info(lengths, local_index)
     local_heads = queries.shape[1] // HD
-    partial_value = jnp.dot(tokens, kv_weight, preferred_element_type=jnp.float32)
-    pieces = partial_value.astype(jnp.bfloat16).reshape(rows, tp_size, HD)
-    arrived = lax.all_to_all(jnp.transpose(pieces, (1, 0, 2)), "tp", 0, 0, tiled=True)
-    own = jnp.sum(arrived.astype(jnp.float32), axis=0)
+    pieces = jnp.stack([
+        jnp.dot(tokens, kv_weight[:, block * HD : (block + 1) * HD], preferred_element_type=jnp.float32)
+        for block in range(tp_size)
+    ])
+    arrived = lax.all_to_all(pieces, "tp", 0, 0, tiled=True)
+    own = jnp.sum(arrived, axis=0)
     is_key = tp_index % 2 == 0
     turned = rotate(own.reshape(rows, 1, HD), positions).reshape(rows, HD)
     mine = jnp.where(is_key, turned, own).astype(jnp.bfloat16)

time: 65.3 us -> 78.9 us (1.21)
  matrix products: 3.11 us -> 12.4 us
  waiting for transfers between devices: 19.3 us -> 26.8 us
  starting transfers between devices: 35.3 us -> 33.4 us
  local copies, waits for them, and re-layouts: 4.35 us -> 2.98 us
    dot_general x1 -> x8, matrix products: 1.41 us -> 10.7 us  [layer(): jnp.dot(tokens, kv_weight[:, block * HD:(block + 1) * HD], preferred_elem...]
    all_to_all x1, waiting for transfers between devices: 8.8 us -> 16.3 us  [layer(): arrived = lax.all_to_all(pieces, 'tp', 0, 0, tiled=True)]
    ppermute x3, starting transfers between devices: 12.2 us -> 10.3 us  [shifted(): lax.ppermute(value, axis, [(source, source + steps) for source in range(f...]
    unnamed x13 -> x15, local copies, waits for them, and re-layouts: 3.36 us -> 2.73 us
  transfers between devices with their start and end apart: 6 -> 6, of which waited for: 3 -> 3; matrix products, arithmetic and copies ran while one was open for 7% -> 6% of each run, Pallas kernels for 0% -> 0%
where the time goes in v8:
time: 78.9 us; the launch traced here: 78.4 us
  starting transfers between devices  33.4 us (42%)
  waiting for transfers between devices  26.8 us (34%)
  matrix products  12.4 us (16%)
  local copies, waits for them, and re-layouts  2.98 us (4%)
  other arithmetic  1.98 us (3%)
  between operations  0.88 us (1%)
    all_to_all x1, waiting for transfers between devices, layer(): arrived = lax.all_to_all(pieces, 'tp', 0, 0, tiled=True)  16.3 us
    all_to_all x1, starting transfers between devices, layer(): arrived = lax.all_to_all(pieces, 'tp', 0, 0, tiled=True)  10.9 us
    dot_general x8, matrix products, layer(): jnp.dot(tokens, kv_weight[:, block * HD:(block + 1) * HD], preferred_elem...  10.7 us
    all_to_all x1, starting transfers between devices, layer(): cache = lax.all_to_all(outgoing, 'req', 0, 0, tiled=True)  10.3 us
    ppermute x3, starting transfers between devices, shifted(): lax.ppermute(value, axis, [(source, source + steps) for source in range(f...  10.3 us
    all_to_all x1, waiting for transfers between devices, layer(): cache = lax.all_to_all(outgoing, 'req', 0, 0, tiled=True)  7.99 us
    unnamed x15, local copies, waits for them, and re-layouts  2.73 us
    ppermute x1, waiting for transfers between devices, layer(): other = lax.ppermute(mine, 'tp', [(i, i ^ 1) for i in range(tp_size)])  2.51 us
  transfers between devices with their start and end apart: 6, of which 3 were waited for; matrix products, arithmetic and copies ran while one was open for 6% of the time, Pallas kernels for 0%

profile of v8, /device:TPU:1, one launch (start us, length us, event | category | flops | bytes accessed | tf_op | source)
XLA Modules:
  0.0 78.4 jit_solution(9512857450160533314)
XLA Ops:
  0.6 0.0 copy-start
  0.6 0.0 copy-start.1
  0.7 0.9 %copy-done = bf16[128,1024]{1,0:T(8,128)(2,1)S(1)} copy-done((bf16[128,1024]{1,0:T(8,128)(2,1)S(1)}, bf16[128,1024]{1,0:T(8,128)(2,1)}, u32[]{:S(2)}) %copy-start) | copy-done | bytes 262168
  1.6 1.8 %fusion.9 = f32[8,128,128]{2,1,0:T(8,128)} fusion(bf16[128,1024]{1,0:T(8,128)(2,1)S(1)} %copy-done, bf16[1024,1024]{1,0:T(8,128)(2,1)} %param.6), kind=kOutput, calls=%fused_computation.20 | convolution fusion | flops 33554432 | bytes 589824 | tf_op jit(solution)/shard_map/dot_general | solution.py:52
  3.4 1.8 %fusion.8 = f32[8,128,128]{2,1,0:T(8,128)} fusion(f32[8,128,128]{2,1,0:T(8,128)} %fusion.9, bf16[128,1024]{1,0:T(8,128)(2,1)S(1)} %copy-done, bf16[1024,1024]{1,0:T(8,128)(2,1)} %param.6), kind=kOutput, calls=%fused_computation.18 | convolution fusion | flops 33554432 | bytes 589824 | tf_op jit(solution)/shard_map/dot_general | solution.py:52
  5.2 1.8 %fusion.7 = f32[8,128,128]{2,1,0:T(8,128)} fusion(f32[8,128,128]{2,1,0:T(8,128)} %fusion.8, bf16[128,1024]{1,0:T(8,128)(2,1)S(1)} %copy-done, bf16[1024,1024]{1,0:T(8,128)(2,1)} %param.6), kind=kOutput, calls=%fused_computation.16 | convolution fusion | flops 33554432 | bytes 589824 | tf_op jit(solution)/shard_map/dot_general | solution.py:52
  6.9 1.8 %fusion.6 = f32[8,128,128]{2,1,0:T(8,128)} fusion(f32[8,128,128]{2,1,0:T(8,128)} %fusion.7, bf16[128,1024]{1,0:T(8,128)(2,1)S(1)} %copy-done, bf16[1024,1024]{1,0:T(8,128)(2,1)} %param.6), kind=kOutput, calls=%fused_computation.14 | convolution fusion | flops 33554432 | bytes 589824 | tf_op jit(solution)/shard_map/dot_general | solution.py:52
  8.8 0.0 copy-done.1
  8.8 0.9 %fusion.5 = f32[8,128,128]{2,1,0:T(8,128)} fusion(f32[8,128,128]{2,1,0:T(8,128)} %fusion.6, bf16[128,1024]{1,0:T(8,128)(2,1)S(1)} %copy-done, bf16[1024,1024]{1,0:T(8,128)(2,1)S(1)} %copy-done.1), kind=kOutput, calls=%fused_computation.12 | convolution fusion | flops 33554432 | bytes 589824 | tf_op jit(solution)/shard_map/dot_general | solution.py:52
  9.6 0.9 %fusion.4 = f32[8,128,128]{2,1,0:T(8,128)} fusion(f32[8,128,128]{2,1,0:T(8,128)} %fusion.5, bf16[128,1024]{1,0:T(8,128)(2,1)S(1)} %copy-done, bf16[1024,1024]{1,0:T(8,128)(2,1)S(1)} %copy-done.1), kind=kOutput, calls=%fused_computation.10 | convolution fusion | flops 33554432 | bytes 589824 | tf_op jit(solution)/shard_map/dot_general | solution.py:52
  10.5 0.9 %fusion.3 = f32[8,128,128]{2,1,0:T(8,128)} fusion(f32[8,128,128]{2,1,0:T(8,128)} %fusion.4, bf16[128,1024]{1,0:T(8,128)(2,1)S(1)} %copy-done, bf16[1024,1024]{1,0:T(8,128)(2,1)S(1)} %copy-done.1), kind=kOutput, calls=%fused_computation.8 | convolution fusion | flops 33554432 | bytes 589824 | tf_op jit(solution)/shard_map/dot_general | solution.py:52
  11.4 0.9 %fusion.2 = f32[8,128,128]{2,1,0:T(8,128)} fusion(f32[8,128,128]{2,1,0:T(8,128)} %fusion.3, bf16[128,1024]{1,0:T(8,128)(2,1)S(1)} %copy-done, bf16[1024,1024]{1,0:T(8,128)(2,1)S(1)} %copy-done.1), kind=kOutput, calls=%fused_computation.6 | convolution fusion | flops 33554432 | bytes 589824 | tf_op jit(solution)/shard_map/dot_general | solution.py:52
  12.2 10.9 %all-to-all-start = ((f32[8,128,128]{2,1,0:T(8,128)}), f32[8,128,128]{2,1,0:T(8,128)S(1)}, u32[]{:S(2)}, u32[]{:S(2)}) async-start(f32[8,128,128]{2,1,0:T(8,128)} %fusion.2), calls=%async_computation | async-start | bytes 1048576 | tf_op jit(solution)/shard_map/all_to_all | solution.py:55
  23.2 0.0 copy-done.3
  23.2 0.1 copy.16
  23.3 0.1 reduce-window.8
  23.3 0.1 reduce
  23.4 0.0 copy-done.2
  23.5 0.1 copy.17
  23.6 0.1 copy.24
  23.7 0.1 copy.25
  23.9 0.1 fusion.36
  24.0 0.1 convert_reduce_fusion
  24.1 0.2 convert_reduce_fusion.1
  24.3 0.1 compare_and_fusion
  24.4 0.3 multiply_cosine_fusion.1
  24.7 0.1 subtract_convert_fusion
  24.8 16.3 %all-to-all-done = f32[8,128,128]{2,1,0:T(8,128)S(1)} async-done(((f32[8,128,128]{2,1,0:T(8,128)}), f32[8,128,128]{2,1,0:T(8,128)S(1)}, u32[]{:S(2)}, u32[]{:S(2)}) %all-to-all-start) | async-done | bytes 524320 | tf_op jit(solution)/shard_map/all_to_all | solution.py:55
  41.1 0.3 fusion.29
  41.4 0.1 fusion.32
  41.5 1.9 %collective-permute-start = (bf16[128,128]{1,0:T(8,128)(2,1)S(1)}, bf16[128,128]{1,0:T(8,128)(2,1)S(1)}, u32[]{:S(2)}, u32[]{:S(2)}) collective-permute-start(bf16[128,128]{1,0:T(8,128)(2,1)S(1)} %fusion.32), channel_id=1, source_target_pairs={{0,1},{1,0},{2,3},{3,2},{4,5},{5,4},{6,7},{7,6},{8,9},{9,8},{10,11... | collective-permute-start | bytes 98312 | tf_op jit(solution)/shard_map/ppermute | solution.py:60
  43.4 0.1 iota_add_fusion
  43.5 0.1 add.79
  43.7 2.5 %collective-permute-done = bf16[128,128]{1,0:T(8,128)(2,1)S(1)} collective-permute-done((bf16[128,128]{1,0:T(8,128)(2,1)S(1)}, bf16[128,128]{1,0:T(8,128)(2,1)S(1)}, u32[]{:S(2)}, u32[]{:S(2)}) %collective-permute-start) | collective-permute-done | bytes 32800 | tf_op jit(solution)/shard_map/ppermute | solution.py:60
  46.2 6.2 %collective-permute-start.1 = (bf16[128,256]{1,0:T(8,128)(2,1)S(1)}, bf16[128,256]{1,0:T(8,128)(2,1)S(1)}, u32[]{:S(2)}, u32[]{:S(2)}) collective-permute-start(bf16[128,256]{1,0:T(8,128)(2,1)S(1)} %pad_maximum_fusion), channel_id=1, source_target_pairs={{0,24},{8,32},{16,40},{24,48},{32,56},{40,64},{48,72},{56,80},{64,... | collective-permute-start | bytes 196616 | tf_op jit(solution)/shard_map/ppermute | solution.py:19
  52.4 2.2 %collective-permute-start.2 = (bf16[128,256]{1,0:T(8,128)(2,1)S(1)}, bf16[128,256]{1,0:T(8,128)(2,1)S(1)}, u32[]{:S(2)}, u32[]{:S(2)}) collective-permute-start(bf16[128,256]{1,0:T(8,128)(2,1)S(1)} %pad_maximum_fusion), channel_id=1, source_target_pairs={{0,16},{8,24},{16,32},{24,40},{32,48},{40,56},{48,64},{56,72},{64,... | collective-permute-start | bytes 196616 | tf_op jit(solution)/shard_map/ppermute | solution.py:19
  54.6 1.9 %collective-permute-start.3 = (bf16[128,256]{1,0:T(8,128)(2,1)S(1)}, bf16[128,256]{1,0:T(8,128)(2,1)S(1)}, u32[]{:S(2)}, u32[]{:S(2)}) collective-permute-start(bf16[128,256]{1,0:T(8,128)(2,1)S(1)} %pad_maximum_fusion), channel_id=1, source_target_pairs={{0,8},{8,16},{16,24},{24,32},{32,40},{40,48},{48,56},{56,64},{64,7... | collective-permute-start | bytes 196616 | tf_op jit(solution)/shard_map/ppermute | solution.py:19
  56.6 0.8 %convolution_convert_fusion = bf16[256,128]{1,0:T(8,128)(2,1)} fusion(bf16[128,128]{1,0:T(8,128)(2,1)S(1)} %fusion.32, s32[128]{0:T(128)S(1)} %add.79), kind=kOutput, calls=%fused_computation.4 | convolution fusion | flops 8454144 | bytes 98816 | tf_op jit(solution)/shard_map/dot_general | solution.py:103
  57.3 10.3 %all-to-all-start.1 = ((bf16[64,4,128]{2,1,0:T(4,128)(2,1)}), bf16[64,4,128]{2,1,0:T(4,128)(2,1)S(1)}, u32[]{:S(2)}, u32[]{:S(2)}) async-start(bf16[64,4,128]{2,1,0:T(4,128)(2,1)} %bitcast.19), calls=%async_computation.1 | async-start | bytes 131072 | tf_op jit(solution)/shard_map/all_to_all | solution.py:104
  67.7 0.0 collective-permute-done.1
  67.7 0.0 collective-permute-done.2
  67.7 0.0 collective-permute-done.3
  67.8 0.5 fusion.41
  68.2 0.3 fusion.10
  68.6 0.5 fusion.1
  69.0 0.8 copy.21
  69.8 8.0 %all-to-all-done.1 = bf16[64,4,128]{2,1,0:T(4,128)(2,1)S(1)} async-done(((bf16[64,4,128]{2,1,0:T(4,128)(2,1)}), bf16[64,4,128]{2,1,0:T(4,128)(2,1)S(1)}, u32[]{:S(2)}, u32[]{:S(2)}) %all-to-all-start.1) | async-done | bytes 65568 | tf_op jit(solution)/shard_map/all_to_all | solution.py:104
  77.8 0.6 copy.34
  (15 shorter events, 0.1 us)
Async XLA Ops:
  0.6 1.0 %copy-start = (bf16[128,1024]{1,0:T(8,128)(2,1)S(1)}, bf16[128,1024]{1,0:T(8,128)(2,1)}, u32[]{:S(2)}) copy-start(bf16[128,1024]{1,0:T(8,128)(2,1)} %param.5) | copy-start | bytes 786436
  0.6 8.1 %copy-start.1 = (bf16[1024,1024]{1,0:T(8,128)(2,1)S(1)}, bf16[1024,1024]{1,0:T(8,128)(2,1)}, u32[]{:S(2)}) copy-start(bf16[1024,1024]{1,0:T(8,128)(2,1)} %param.6) | copy-start | bytes 6291460
  6.9 16.2 %copy-start.3 = (s32[32]{0:T(128)S(1)}, s32[32]{0:T(128)}, u32[]{:S(2)}) copy-start(s32[32]{0:T(128)} %param.8) | copy-start | bytes 388
  6.9 16.5 %copy-start.2 = (bf16[128,512]{1,0:T(8,128)(2,1)S(1)}, bf16[128,512]{1,0:T(8,128)(2,1)}, u32[]{:S(2)}) copy-start(bf16[128,512]{1,0:T(8,128)(2,1)} %param.7) | copy-start | bytes 393220
  10.5 13.6 %copy-start.4 = (s32[64,1]{0,1:T(1,128)S(1)}, s32[64,1]{0,1:T(1,128)}, u32[]{:S(2)}) copy-start(s32[64,1]{0,1:T(1,128)} %param.9) | copy-start | bytes 772
  12.2 28.8 %all-to-all-start = ((f32[8,128,128]{2,1,0:T(8,128)}), f32[8,128,128]{2,1,0:T(8,128)S(1)}, u32[]{:S(2)}, u32[]{:S(2)}) async-start(f32[8,128,128]{2,1,0:T(8,128)} %fusion.2), calls=%async_computation | async-start | bytes 1048576 | tf_op jit(solution)/shard_map/all_to_all | solution.py:55
  41.5 4.7 %collective-permute-start = (bf16[128,128]{1,0:T(8,128)(2,1)S(1)}, bf16[128,128]{1,0:T(8,128)(2,1)S(1)}, u32[]{:S(2)}, u32[]{:S(2)}) collective-permute-start(bf16[128,128]{1,0:T(8,128)(2,1)S(1)} %fusion.32), channel_id=1, source_target_pairs={{0,1},{1,0},{2,3},{3,2},{4,5},{5,4},{6,7},{7,6},{8,9},{9,8},{10,11... | collective-permute-start | bytes 98312 | tf_op jit(solution)/shard_map/ppermute | solution.py:60
  46.2 21.5 %collective-permute-start.1 = (bf16[128,256]{1,0:T(8,128)(2,1)S(1)}, bf16[128,256]{1,0:T(8,128)(2,1)S(1)}, u32[]{:S(2)}, u32[]{:S(2)}) collective-permute-start(bf16[128,256]{1,0:T(8,128)(2,1)S(1)} %pad_maximum_fusion), channel_id=1, source_target_pairs={{0,24},{8,32},{16,40},{24,48},{32,56},{40,64},{48,72},{56,80},{64,... | collective-permute-start | bytes 196616 | tf_op jit(solution)/shard_map/ppermute | solution.py:19
  52.4 15.3 %collective-permute-start.2 = (bf16[128,256]{1,0:T(8,128)(2,1)S(1)}, bf16[128,256]{1,0:T(8,128)(2,1)S(1)}, u32[]{:S(2)}, u32[]{:S(2)}) collective-permute-start(bf16[128,256]{1,0:T(8,128)(2,1)S(1)} %pad_maximum_fusion), channel_id=1, source_target_pairs={{0,16},{8,24},{16,32},{24,40},{32,48},{40,56},{48,64},{56,72},{64,... | collective-permute-start | bytes 196616 | tf_op jit(solution)/shard_map/ppermute | solution.py:19
  54.6 13.1 %collective-permute-start.3 = (bf16[128,256]{1,0:T(8,128)(2,1)S(1)}, bf16[128,256]{1,0:T(8,128)(2,1)S(1)}, u32[]{:S(2)}, u32[]{:S(2)}) collective-permute-start(bf16[128,256]{1,0:T(8,128)(2,1)S(1)} %pad_maximum_fusion), channel_id=1, source_target_pairs={{0,8},{8,16},{16,24},{24,32},{32,40},{40,48},{48,56},{56,64},{64,7... | collective-permute-start | bytes 196616 | tf_op jit(solution)/shard_map/ppermute | solution.py:19
  57.3 20.4 %all-to-all-start.1 = ((bf16[64,4,128]{2,1,0:T(4,128)(2,1)}), bf16[64,4,128]{2,1,0:T(4,128)(2,1)S(1)}, u32[]{:S(2)}, u32[]{:S(2)}) async-start(bf16[64,4,128]{2,1,0:T(4,128)(2,1)} %bitcast.19), calls=%async_computation.1 | async-start | bytes 131072 | tf_op jit(solution)/shard_map/all_to_all | solution.py:104

commit v9 on v6

--- a/solution.py
+++ b/solution.py
@@ -49,9 +49,9 @@
     segment, positions = segment_info(lengths, local_index)
     local_heads = queries.shape[1] // HD
     partial_value = jnp.dot(tokens, kv_weight, preferred_element_type=jnp.float32)
-    pieces = partial_value.astype(jnp.bfloat16).reshape(rows, tp_size, HD)
+    pieces = partial_value.reshape(rows, tp_size, HD)
     arrived = lax.all_to_all(jnp.transpose(pieces, (1, 0, 2)), "tp", 0, 0, tiled=True)
-    own = jnp.sum(arrived.astype(jnp.float32), axis=0)
+    own = jnp.sum(arrived, axis=0)
     is_key = tp_index % 2 == 0
     turned = rotate(own.reshape(rows, 1, HD), positions).reshape(rows, HD)
     mine = jnp.where(is_key, turned, own).astype(jnp.bfloat16)
@@ -98,6 +98,7 @@
     slots = lax.axis_size("req") * capacity
     row_target = (target[:, None] * page_rows + jnp.arange(page_rows, dtype=jnp.int32)[None, :]).reshape(rows)
     placing = (jnp.arange(slots * page_rows, dtype=jnp.int32)[:, None] == row_target[None, :]).astype(jnp.bfloat16)
+    placing = lax.optimization_barrier(placing)
     outgoing = jnp.dot(placing, mine, preferred_element_type=jnp.float32).astype(jnp.bfloat16)
     cache = lax.all_to_all(outgoing, "req", 0, 0, tiled=True)
     return (attended, cache)

time: 65.3 us -> 71 us (1.087)
  waiting for transfers between devices: 19.3 us -> 26.7 us
  starting transfers between devices: 35.3 us -> 33.4 us
    all_to_all x1, waiting for transfers between devices: 8.8 us -> 16 us  [layer(): lax.all_to_all(jnp.transpose(pieces, (1, 0, 2)), 'tp', 0, 0, tiled=True)]
    ppermute x3, starting transfers between devices: 12.2 us -> 10.3 us  [shifted(): lax.ppermute(value, axis, [(source, source + steps) for source in range(f...]
where the time goes in v9:
time: 71 us; the launch traced here: 70.6 us
  starting transfers between devices  33.4 us (47%)
  waiting for transfers between devices  26.7 us (38%)
  local copies, waits for them, and re-layouts  4.44 us (6%)
  matrix products  3.09 us (4%)
  other arithmetic  2 us (3%)
  between operations  0.91 us (1%)
    all_to_all x1, waiting for transfers between devices, layer(): lax.all_to_all(jnp.transpose(pieces, (1, 0, 2)), 'tp', 0, 0, tiled=True)  16 us
    all_to_all x1, starting transfers between devices, layer(): lax.all_to_all(jnp.transpose(pieces, (1, 0, 2)), 'tp', 0, 0, tiled=True)  10.9 us
    all_to_all x1, starting transfers between devices, layer(): cache = lax.all_to_all(outgoing, 'req', 0, 0, tiled=True)  10.3 us
    ppermute x3, starting transfers between devices, shifted(): lax.ppermute(value, axis, [(source, source + steps) for source in range(f...  10.3 us
    all_to_all x1, waiting for transfers between devices, layer(): cache = lax.all_to_all(outgoing, 'req', 0, 0, tiled=True)  7.99 us
    unnamed x13, local copies, waits for them, and re-layouts  3.36 us
    ppermute x1, waiting for transfers between devices, layer(): other = lax.ppermute(mine, 'tp', [(i, i ^ 1) for i in range(tp_size)])  2.7 us
    ppermute x1, starting transfers between devices, layer(): other = lax.ppermute(mine, 'tp', [(i, i ^ 1) for i in range(tp_size)])  1.92 us
  transfers between devices with their start and end apart: 6, of which 3 were waited for; matrix products, arithmetic and copies ran while one was open for 7% of the time, Pallas kernels for 0%

profile of v9, /device:TPU:1, one launch (start us, length us, event | category | flops | bytes accessed | tf_op | source)
XLA Modules:
  0.0 70.6 jit_solution(14154121373666649612)
XLA Ops:
  0.6 0.0 copy-start
  0.6 0.0 copy-start.2
  0.7 0.0 copy-start.1
  0.7 1.6 %copy-done = bf16[1024,1024]{1,0:T(8,128)(2,1)S(1)} copy-done((bf16[1024,1024]{1,0:T(8,128)(2,1)S(1)}, bf16[1024,1024]{1,0:T(8,128)(2,1)}, u32[]{:S(2)}) %copy-start) | copy-done | bytes 2097176
  2.2 1.4 %convolution_bitcast_fusion = f32[16,8,8,128]{3,2,1,0:T(8,128)S(1)} fusion(bf16[128,1024]{1,0:T(8,128)(2,1)} %param.5, bf16[1024,1024]{1,0:T(8,128)(2,1)S(1)} %copy-done), kind=kOutput, calls=%fused_computation.2 | convolution fusion | flops 268435456 | bytes 2883584 | tf_op jit(solution)/shard_map/dot_general | solution.py:51
  3.6 0.0 copy-start.3
  3.6 0.8 %copy.36 = f32[16,8,8,128]{3,2,0,1:T(8,128)} copy(f32[16,8,8,128]{3,2,1,0:T(8,128)S(1)} %convolution_bitcast_fusion) | data formatting | bytes 1048576 | tf_op jit(solution)/shard_map/reshape | solution.py:52
  4.5 10.9 %all-to-all-start = ((f32[8,128,128]{2,1,0:T(8,128)}), f32[8,128,128]{2,1,0:T(8,128)S(1)}, u32[]{:S(2)}, u32[]{:S(2)}) async-start(f32[8,128,128]{2,1,0:T(8,128)} %bitcast.41), calls=%async_computation | async-start | bytes 1048576 | tf_op jit(solution)/shard_map/all_to_all | solution.py:53
  15.4 0.0 copy-done.2
  15.4 0.1 copy.23
  15.5 0.1 reduce-window.8
  15.5 0.1 reduce
  15.7 0.0 copy-done.1
  15.7 0.1 copy.24
  15.8 0.1 copy.32
  15.9 0.1 copy.33
  16.1 0.1 fusion.20
  16.2 0.1 convert_reduce_fusion
  16.3 0.0 copy-done.3
  16.3 0.2 convert_reduce_fusion.1
  16.5 0.1 iota_add_fusion
  16.5 0.1 add.79
  16.7 0.1 compare_and_fusion
  16.8 0.3 multiply_cosine_fusion.1
  17.2 0.1 subtract_convert_fusion
  17.2 16.0 %all-to-all-done = f32[8,128,128]{2,1,0:T(8,128)S(1)} async-done(((f32[8,128,128]{2,1,0:T(8,128)}), f32[8,128,128]{2,1,0:T(8,128)S(1)}, u32[]{:S(2)}, u32[]{:S(2)}) %all-to-all-start) | async-done | bytes 524320 | tf_op jit(solution)/shard_map/all_to_all | solution.py:53
  33.3 0.3 fusion.14
  33.6 0.1 fusion.17
  33.7 1.9 %collective-permute-start = (bf16[128,128]{1,0:T(8,128)(2,1)S(1)}, bf16[128,128]{1,0:T(8,128)(2,1)S(1)}, u32[]{:S(2)}, u32[]{:S(2)}) collective-permute-start(bf16[128,128]{1,0:T(8,128)(2,1)S(1)} %fusion.17), channel_id=1, source_target_pairs={{0,1},{1,0},{2,3},{3,2},{4,5},{5,4},{6,7},{7,6},{8,9},{9,8},{10,11... | collective-permute-start | bytes 98312 | tf_op jit(solution)/shard_map/ppermute | solution.py:58
  35.7 2.7 %collective-permute-done = bf16[128,128]{1,0:T(8,128)(2,1)S(1)} collective-permute-done((bf16[128,128]{1,0:T(8,128)(2,1)S(1)}, bf16[128,128]{1,0:T(8,128)(2,1)S(1)}, u32[]{:S(2)}, u32[]{:S(2)}) %collective-permute-start) | collective-permute-done | bytes 32800 | tf_op jit(solution)/shard_map/ppermute | solution.py:58
  38.4 6.2 %collective-permute-start.1 = (bf16[128,256]{1,0:T(8,128)(2,1)S(1)}, bf16[128,256]{1,0:T(8,128)(2,1)S(1)}, u32[]{:S(2)}, u32[]{:S(2)}) collective-permute-start(bf16[128,256]{1,0:T(8,128)(2,1)S(1)} %pad_maximum_fusion), channel_id=1, source_target_pairs={{0,24},{8,32},{16,40},{24,48},{32,56},{40,64},{48,72},{56,80},{64,... | collective-permute-start | bytes 196616 | tf_op jit(solution)/shard_map/ppermute | solution.py:19
  44.6 2.2 %collective-permute-start.2 = (bf16[128,256]{1,0:T(8,128)(2,1)S(1)}, bf16[128,256]{1,0:T(8,128)(2,1)S(1)}, u32[]{:S(2)}, u32[]{:S(2)}) collective-permute-start(bf16[128,256]{1,0:T(8,128)(2,1)S(1)} %pad_maximum_fusion), channel_id=1, source_target_pairs={{0,16},{8,24},{16,32},{24,40},{32,48},{40,56},{48,64},{56,72},{64,... | collective-permute-start | bytes 196616 | tf_op jit(solution)/shard_map/ppermute | solution.py:19
  46.8 1.9 %collective-permute-start.3 = (bf16[128,256]{1,0:T(8,128)(2,1)S(1)}, bf16[128,256]{1,0:T(8,128)(2,1)S(1)}, u32[]{:S(2)}, u32[]{:S(2)}) collective-permute-start(bf16[128,256]{1,0:T(8,128)(2,1)S(1)} %pad_maximum_fusion), channel_id=1, source_target_pairs={{0,8},{8,16},{16,24},{24,32},{32,40},{40,48},{48,56},{56,64},{64,7... | collective-permute-start | bytes 196616 | tf_op jit(solution)/shard_map/ppermute | solution.py:19
  48.8 0.8 %convolution_convert_fusion = bf16[256,128]{1,0:T(8,128)(2,1)} fusion(bf16[256,128]{1,0:T(8,128)(2,1)S(1)} %fusion.9, bf16[128,128]{1,0:T(8,128)(2,1)S(1)} %fusion.17), kind=kOutput, calls=%fused_computation.5 | convolution fusion | flops 8421376 | bytes 163840 | tf_op jit(solution)/shard_map/dot_general | solution.py:102
  49.5 10.3 %all-to-all-start.1 = ((bf16[64,4,128]{2,1,0:T(4,128)(2,1)}), bf16[64,4,128]{2,1,0:T(4,128)(2,1)S(1)}, u32[]{:S(2)}, u32[]{:S(2)}) async-start(bf16[64,4,128]{2,1,0:T(4,128)(2,1)} %bitcast.12), calls=%async_computation.1 | async-start | bytes 131072 | tf_op jit(solution)/shard_map/all_to_all | solution.py:103
  59.9 0.0 collective-permute-done.1
  59.9 0.0 collective-permute-done.2
  59.9 0.0 collective-permute-done.3
  60.0 0.5 fusion.25
  60.4 0.3 fusion.2
  60.8 0.5 fusion.1
  61.2 0.8 %copy.29 = bf16[128,512]{1,0:T(8,128)(2,1)} copy(bf16[128,512]{0,1:T(8,128)(2,1)S(1)} %bitcast.45) | data formatting | bytes 262144
  62.0 8.0 %all-to-all-done.1 = bf16[64,4,128]{2,1,0:T(4,128)(2,1)S(1)} async-done(((bf16[64,4,128]{2,1,0:T(4,128)(2,1)}), bf16[64,4,128]{2,1,0:T(4,128)(2,1)S(1)}, u32[]{:S(2)}, u32[]{:S(2)}) %all-to-all-start.1) | async-done | bytes 65568 | tf_op jit(solution)/shard_map/all_to_all | solution.py:103
  70.0 0.6 copy.38
  (12 shorter events, 0.2 us)
Async XLA Ops:
  0.6 1.6 %copy-start = (bf16[1024,1024]{1,0:T(8,128)(2,1)S(1)}, bf16[1024,1024]{1,0:T(8,128)(2,1)}, u32[]{:S(2)}) copy-start(bf16[1024,1024]{1,0:T(8,128)(2,1)} %param.6) | copy-start | bytes 6291460
  0.6 14.7 %copy-start.2 = (s32[32]{0:T(128)S(1)}, s32[32]{0:T(128)}, u32[]{:S(2)}) copy-start(s32[32]{0:T(128)} %param.8) | copy-start | bytes 388
  0.7 15.0 %copy-start.1 = (bf16[128,512]{1,0:T(8,128)(2,1)S(1)}, bf16[128,512]{1,0:T(8,128)(2,1)}, u32[]{:S(2)}) copy-start(bf16[128,512]{1,0:T(8,128)(2,1)} %param.7) | copy-start | bytes 393220
  3.6 12.6 %copy-start.3 = (s32[64,1]{0,1:T(1,128)S(1)}, s32[64,1]{0,1:T(1,128)}, u32[]{:S(2)}) copy-start(s32[64,1]{0,1:T(1,128)} %param.9) | copy-start | bytes 772
  4.5 28.8 %all-to-all-start = ((f32[8,128,128]{2,1,0:T(8,128)}), f32[8,128,128]{2,1,0:T(8,128)S(1)}, u32[]{:S(2)}, u32[]{:S(2)}) async-start(f32[8,128,128]{2,1,0:T(8,128)} %bitcast.41), calls=%async_computation | async-start | bytes 1048576 | tf_op jit(solution)/shard_map/all_to_all | solution.py:53
  33.7 4.7 %collective-permute-start = (bf16[128,128]{1,0:T(8,128)(2,1)S(1)}, bf16[128,128]{1,0:T(8,128)(2,1)S(1)}, u32[]{:S(2)}, u32[]{:S(2)}) collective-permute-start(bf16[128,128]{1,0:T(8,128)(2,1)S(1)} %fusion.17), channel_id=1, source_target_pairs={{0,1},{1,0},{2,3},{3,2},{4,5},{5,4},{6,7},{7,6},{8,9},{9,8},{10,11... | collective-permute-start | bytes 98312 | tf_op jit(solution)/shard_map/ppermute | solution.py:58
  38.4 21.5 %collective-permute-start.1 = (bf16[128,256]{1,0:T(8,128)(2,1)S(1)}, bf16[128,256]{1,0:T(8,128)(2,1)S(1)}, u32[]{:S(2)}, u32[]{:S(2)}) collective-permute-start(bf16[128,256]{1,0:T(8,128)(2,1)S(1)} %pad_maximum_fusion), channel_id=1, source_target_pairs={{0,24},{8,32},{16,40},{24,48},{32,56},{40,64},{48,72},{56,80},{64,... | collective-permute-start | bytes 196616 | tf_op jit(solution)/shard_map/ppermute | solution.py:19
  44.6 15.3 %collective-permute-start.2 = (bf16[128,256]{1,0:T(8,128)(2,1)S(1)}, bf16[128,256]{1,0:T(8,128)(2,1)S(1)}, u32[]{:S(2)}, u32[]{:S(2)}) collective-permute-start(bf16[128,256]{1,0:T(8,128)(2,1)S(1)} %pad_maximum_fusion), channel_id=1, source_target_pairs={{0,16},{8,24},{16,32},{24,40},{32,48},{40,56},{48,64},{56,72},{64,... | collective-permute-start | bytes 196616 | tf_op jit(solution)/shard_map/ppermute | solution.py:19
  46.8 13.1 %collective-permute-start.3 = (bf16[128,256]{1,0:T(8,128)(2,1)S(1)}, bf16[128,256]{1,0:T(8,128)(2,1)S(1)}, u32[]{:S(2)}, u32[]{:S(2)}) collective-permute-start(bf16[128,256]{1,0:T(8,128)(2,1)S(1)} %pad_maximum_fusion), channel_id=1, source_target_pairs={{0,8},{8,16},{16,24},{24,32},{32,40},{40,48},{48,56},{56,64},{64,7... | collective-permute-start | bytes 196616 | tf_op jit(solution)/shard_map/ppermute | solution.py:19
  49.5 20.4 %all-to-all-start.1 = ((bf16[64,4,128]{2,1,0:T(4,128)(2,1)}), bf16[64,4,128]{2,1,0:T(4,128)(2,1)S(1)}, u32[]{:S(2)}, u32[]{:S(2)}) async-start(bf16[64,4,128]{2,1,0:T(4,128)(2,1)} %bitcast.12), calls=%async_computation.1 | async-start | bytes 131072 | tf_op jit(solution)/shard_map/all_to_all | solution.py:103

commit v10 on v9

--- a/solution.py
+++ b/solution.py
@@ -82,11 +82,11 @@
     largest = jnp.max(scores, axis=2, keepdims=True)
     weights = jnp.exp(scores - largest)
     total = jnp.sum(weights, axis=2, keepdims=True)
-    mixed = lax.dot_general(
-        weights.astype(jnp.bfloat16), value_head, (((2,), (0,)), ((), ())),
+    mixed = jnp.dot(
+        weights.astype(jnp.bfloat16).reshape(rows * local_heads, key_total), value_head,
         preferred_element_type=jnp.float32,
     )
-    attended = (mixed / total).astype(jnp.bfloat16).reshape(rows, local_heads * HD)
+    attended = (mixed / total.reshape(rows * local_heads, 1)).astype(jnp.bfloat16).reshape(rows, local_heads * HD)
     pages_here = page_owner.shape[0]
     owners = page_owner[:, 0]
     page_rows = rows // pages_here
@@ -98,7 +98,6 @@
     slots = lax.axis_size("req") * capacity
     row_target = (target[:, None] * page_rows + jnp.arange(page_rows, dtype=jnp.int32)[None, :]).reshape(rows)
     placing = (jnp.arange(slots * page_rows, dtype=jnp.int32)[:, None] == row_target[None, :]).astype(jnp.bfloat16)
-    placing = lax.optimization_barrier(placing)
     outgoing = jnp.dot(placing, mine, preferred_element_type=jnp.float32).astype(jnp.bfloat16)
     cache = lax.all_to_all(outgoing, "req", 0, 0, tiled=True)
     return (attended, cache)

time: 71 us -> 71 us (level)
  local copies, waits for them, and re-layouts: 4.44 us -> 5.16 us
    reshape x0 -> x2, local copies, waits for them, and re-layouts: none -> 0.87 us  [the longest x1 0.74 us: layer(): (mixed / total.reshape(rows * local_heads, 1)).astype(jnp.bfloat16)]
    unnamed x13 -> x12, local copies, waits for them, and re-layouts: 3.36 us -> 2.59 us
where the time goes in v10:
time: 71 us; the launch traced here: 70.6 us
  starting transfers between devices  33.4 us (47%)
  waiting for transfers between devices  26.4 us (37%)
  local copies, waits for them, and re-layouts  5.16 us (7%)
  matrix products  3.09 us (4%)
  other arithmetic  1.64 us (2%)
  between operations  0.91 us (1%)
    all_to_all x1, waiting for transfers between devices, layer(): lax.all_to_all(jnp.transpose(pieces, (1, 0, 2)), 'tp', 0, 0, tiled=True)  16.3 us
    all_to_all x1, starting transfers between devices, layer(): lax.all_to_all(jnp.transpose(pieces, (1, 0, 2)), 'tp', 0, 0, tiled=True)  10.9 us
    all_to_all x1, starting transfers between devices, layer(): cache = lax.all_to_all(outgoing, 'req', 0, 0, tiled=True)  10.3 us
    ppermute x3, starting transfers between devices, shifted(): lax.ppermute(value, axis, [(source, source + steps) for source in range(f...  10.3 us
    all_to_all x1, waiting for transfers between devices, layer(): cache = lax.all_to_all(outgoing, 'req', 0, 0, tiled=True)  7.6 us
    unnamed x12, local copies, waits for them, and re-layouts  2.59 us
    ppermute x1, waiting for transfers between devices, layer(): other = lax.ppermute(mine, 'tp', [(i, i ^ 1) for i in range(tp_size)])  2.51 us
    ppermute x1, starting transfers between devices, layer(): other = lax.ppermute(mine, 'tp', [(i, i ^ 1) for i in range(tp_size)])  1.92 us
  transfers between devices with their start and end apart: 6, of which 3 were waited for; matrix products, arithmetic and copies ran while one was open for 7% of the time, Pallas kernels for 0%

profile of v10, /device:TPU:1, one launch (start us, length us, event | category | flops | bytes accessed | tf_op | source)
XLA Modules:
  0.0 70.6 jit_solution(13138493140753907630)
XLA Ops:
  0.6 0.0 copy-start
  0.6 0.0 copy-start.2
  0.7 0.0 copy-start.1
  0.7 1.6 %copy-done = bf16[1024,1024]{1,0:T(8,128)(2,1)S(1)} copy-done((bf16[1024,1024]{1,0:T(8,128)(2,1)S(1)}, bf16[1024,1024]{1,0:T(8,128)(2,1)}, u32[]{:S(2)}) %copy-start) | copy-done | bytes 2097176
  2.2 1.4 %convolution_bitcast_fusion = f32[16,8,8,128]{3,2,1,0:T(8,128)S(1)} fusion(bf16[128,1024]{1,0:T(8,128)(2,1)} %param.5, bf16[1024,1024]{1,0:T(8,128)(2,1)S(1)} %copy-done), kind=kOutput, calls=%fused_computation.5 | convolution fusion | flops 268435456 | bytes 2883584 | tf_op jit(solution)/shard_map/dot_general | solution.py:51
  3.6 0.0 copy-start.3
  3.6 0.8 %copy.31 = f32[16,8,8,128]{3,2,0,1:T(8,128)} copy(f32[16,8,8,128]{3,2,1,0:T(8,128)S(1)} %convolution_bitcast_fusion) | data formatting | bytes 1048576 | tf_op jit(solution)/shard_map/reshape | solution.py:52
  4.5 10.9 %all-to-all-start = ((f32[8,128,128]{2,1,0:T(8,128)}), f32[8,128,128]{2,1,0:T(8,128)S(1)}, u32[]{:S(2)}, u32[]{:S(2)}) async-start(f32[8,128,128]{2,1,0:T(8,128)} %bitcast.41), calls=%async_computation | async-start | bytes 1048576 | tf_op jit(solution)/shard_map/all_to_all | solution.py:53
  15.4 0.0 copy-done.2
  15.4 0.1 copy.20
  15.5 0.1 reduce-window.8
  15.5 0.1 reduce
  15.7 0.0 copy-done.1
  15.7 0.1 copy.21
  15.8 0.1 copy.27
  15.9 0.1 copy.28
  16.1 0.1 fusion.22
  16.2 0.1 convert_reduce_fusion
  16.3 0.0 copy-done.3
  16.3 0.2 convert_reduce_fusion.1
  16.5 0.1 compare_and_fusion
  16.6 0.3 multiply_cosine_fusion.1
  16.9 0.1 subtract_convert_fusion
  17.0 16.3 %all-to-all-done = f32[8,128,128]{2,1,0:T(8,128)S(1)} async-done(((f32[8,128,128]{2,1,0:T(8,128)}), f32[8,128,128]{2,1,0:T(8,128)S(1)}, u32[]{:S(2)}, u32[]{:S(2)}) %all-to-all-start) | async-done | bytes 524320 | tf_op jit(solution)/shard_map/all_to_all | solution.py:53
  33.3 0.3 fusion.15
  33.6 0.1 fusion.18
  33.7 1.9 %collective-permute-start = (bf16[128,128]{1,0:T(8,128)(2,1)S(1)}, bf16[128,128]{1,0:T(8,128)(2,1)S(1)}, u32[]{:S(2)}, u32[]{:S(2)}) collective-permute-start(bf16[128,128]{1,0:T(8,128)(2,1)S(1)} %fusion.18), channel_id=1, source_target_pairs={{0,1},{1,0},{2,3},{3,2},{4,5},{5,4},{6,7},{7,6},{8,9},{9,8},{10,11... | collective-permute-start | bytes 98312 | tf_op jit(solution)/shard_map/ppermute | solution.py:58
  35.7 0.1 iota_add_fusion
  35.7 0.1 add.79
  35.9 2.5 %collective-permute-done = bf16[128,128]{1,0:T(8,128)(2,1)S(1)} collective-permute-done((bf16[128,128]{1,0:T(8,128)(2,1)S(1)}, bf16[128,128]{1,0:T(8,128)(2,1)S(1)}, u32[]{:S(2)}, u32[]{:S(2)}) %collective-permute-start) | collective-permute-done | bytes 32800 | tf_op jit(solution)/shard_map/ppermute | solution.py:58
  38.4 6.2 %collective-permute-start.1 = (bf16[128,256]{1,0:T(8,128)(2,1)S(1)}, bf16[128,256]{1,0:T(8,128)(2,1)S(1)}, u32[]{:S(2)}, u32[]{:S(2)}) collective-permute-start(bf16[128,256]{1,0:T(8,128)(2,1)S(1)} %pad_maximum_fusion), channel_id=1, source_target_pairs={{0,24},{8,32},{16,40},{24,48},{32,56},{40,64},{48,72},{56,80},{64,... | collective-permute-start | bytes 196616 | tf_op jit(solution)/shard_map/ppermute | solution.py:19
  44.6 2.2 %collective-permute-start.2 = (bf16[128,256]{1,0:T(8,128)(2,1)S(1)}, bf16[128,256]{1,0:T(8,128)(2,1)S(1)}, u32[]{:S(2)}, u32[]{:S(2)}) collective-permute-start(bf16[128,256]{1,0:T(8,128)(2,1)S(1)} %pad_maximum_fusion), channel_id=1, source_target_pairs={{0,16},{8,24},{16,32},{24,40},{32,48},{40,56},{48,64},{56,72},{64,... | collective-permute-start | bytes 196616 | tf_op jit(solution)/shard_map/ppermute | solution.py:19
  46.8 1.9 %collective-permute-start.3 = (bf16[128,256]{1,0:T(8,128)(2,1)S(1)}, bf16[128,256]{1,0:T(8,128)(2,1)S(1)}, u32[]{:S(2)}, u32[]{:S(2)}) collective-permute-start(bf16[128,256]{1,0:T(8,128)(2,1)S(1)} %pad_maximum_fusion), channel_id=1, source_target_pairs={{0,8},{8,16},{16,24},{24,32},{32,40},{40,48},{48,56},{56,64},{64,7... | collective-permute-start | bytes 196616 | tf_op jit(solution)/shard_map/ppermute | solution.py:19
  48.8 0.8 %convolution_convert_fusion = bf16[256,128]{1,0:T(8,128)(2,1)} fusion(bf16[128,128]{1,0:T(8,128)(2,1)S(1)} %fusion.18, s32[128]{0:T(128)S(1)} %add.79), kind=kOutput, calls=%fused_computation.8 | convolution fusion | flops 8454144 | bytes 98816 | tf_op jit(solution)/shard_map/dot_general | solution.py:101
  49.5 10.3 %all-to-all-start.1 = ((bf16[64,4,128]{2,1,0:T(4,128)(2,1)}), bf16[64,4,128]{2,1,0:T(4,128)(2,1)S(1)}, u32[]{:S(2)}, u32[]{:S(2)}) async-start(bf16[64,4,128]{2,1,0:T(4,128)(2,1)} %bitcast.10), calls=%async_computation.1 | async-start | bytes 131072 | tf_op jit(solution)/shard_map/all_to_all | solution.py:102
  59.9 0.0 collective-permute-done.1
  59.9 0.0 collective-permute-done.2
  59.9 0.0 collective-permute-done.3
  60.0 0.6 fusion.33
  60.6 0.4 copy.25
  61.0 0.1 reshape.259
  61.1 0.1 copy.26
  61.2 0.1 div.25
  61.3 0.3 fusion.4
  61.6 0.7 %reshape.260 = bf16[128,512]{1,0:T(8,128)(2,1)} reshape(bf16[512,128]{1,0:T(8,128)(2,1)S(1)} %fusion.4) | data formatting | bytes 262144 | tf_op jit(solution)/shard_map/reshape | solution.py:89
  62.4 7.6 %all-to-all-done.1 = bf16[64,4,128]{2,1,0:T(4,128)(2,1)S(1)} async-done(((bf16[64,4,128]{2,1,0:T(4,128)(2,1)}), bf16[64,4,128]{2,1,0:T(4,128)(2,1)S(1)}, u32[]{:S(2)}, u32[]{:S(2)}) %all-to-all-start.1) | async-done | bytes 65568 | tf_op jit(solution)/shard_map/all_to_all | solution.py:102
  70.0 0.6 copy.33
  (11 shorter events, 0.1 us)
Async XLA Ops:
  0.6 1.6 %copy-start = (bf16[1024,1024]{1,0:T(8,128)(2,1)S(1)}, bf16[1024,1024]{1,0:T(8,128)(2,1)}, u32[]{:S(2)}) copy-start(bf16[1024,1024]{1,0:T(8,128)(2,1)} %param.6) | copy-start | bytes 6291460
  0.6 14.7 %copy-start.2 = (s32[32]{0:T(128)S(1)}, s32[32]{0:T(128)}, u32[]{:S(2)}) copy-start(s32[32]{0:T(128)} %param.8) | copy-start | bytes 388
  0.7 15.0 %copy-start.1 = (bf16[128,512]{1,0:T(8,128)(2,1)S(1)}, bf16[128,512]{1,0:T(8,128)(2,1)}, u32[]{:S(2)}) copy-start(bf16[128,512]{1,0:T(8,128)(2,1)} %param.7) | copy-start | bytes 393220
  3.6 12.6 %copy-start.3 = (s32[64,1]{0,1:T(1,128)S(1)}, s32[64,1]{0,1:T(1,128)}, u32[]{:S(2)}) copy-start(s32[64,1]{0,1:T(1,128)} %param.9) | copy-start | bytes 772
  4.5 28.8 %all-to-all-start = ((f32[8,128,128]{2,1,0:T(8,128)}), f32[8,128,128]{2,1,0:T(8,128)S(1)}, u32[]{:S(2)}, u32[]{:S(2)}) async-start(f32[8,128,128]{2,1,0:T(8,128)} %bitcast.41), calls=%async_computation | async-start | bytes 1048576 | tf_op jit(solution)/shard_map/all_to_all | solution.py:53
  33.7 4.7 %collective-permute-start = (bf16[128,128]{1,0:T(8,128)(2,1)S(1)}, bf16[128,128]{1,0:T(8,128)(2,1)S(1)}, u32[]{:S(2)}, u32[]{:S(2)}) collective-permute-start(bf16[128,128]{1,0:T(8,128)(2,1)S(1)} %fusion.18), channel_id=1, source_target_pairs={{0,1},{1,0},{2,3},{3,2},{4,5},{5,4},{6,7},{7,6},{8,9},{9,8},{10,11... | collective-permute-start | bytes 98312 | tf_op jit(solution)/shard_map/ppermute | solution.py:58
  38.4 21.5 %collective-permute-start.1 = (bf16[128,256]{1,0:T(8,128)(2,1)S(1)}, bf16[128,256]{1,0:T(8,128)(2,1)S(1)}, u32[]{:S(2)}, u32[]{:S(2)}) collective-permute-start(bf16[128,256]{1,0:T(8,128)(2,1)S(1)} %pad_maximum_fusion), channel_id=1, source_target_pairs={{0,24},{8,32},{16,40},{24,48},{32,56},{40,64},{48,72},{56,80},{64,... | collective-permute-start | bytes 196616 | tf_op jit(solution)/shard_map/ppermute | solution.py:19
  44.6 15.3 %collective-permute-start.2 = (bf16[128,256]{1,0:T(8,128)(2,1)S(1)}, bf16[128,256]{1,0:T(8,128)(2,1)S(1)}, u32[]{:S(2)}, u32[]{:S(2)}) collective-permute-start(bf16[128,256]{1,0:T(8,128)(2,1)S(1)} %pad_maximum_fusion), channel_id=1, source_target_pairs={{0,16},{8,24},{16,32},{24,40},{32,48},{40,56},{48,64},{56,72},{64,... | collective-permute-start | bytes 196616 | tf_op jit(solution)/shard_map/ppermute | solution.py:19
  46.8 13.1 %collective-permute-start.3 = (bf16[128,256]{1,0:T(8,128)(2,1)S(1)}, bf16[128,256]{1,0:T(8,128)(2,1)S(1)}, u32[]{:S(2)}, u32[]{:S(2)}) collective-permute-start(bf16[128,256]{1,0:T(8,128)(2,1)S(1)} %pad_maximum_fusion), channel_id=1, source_target_pairs={{0,8},{8,16},{16,24},{24,32},{32,40},{40,48},{48,56},{56,64},{64,7... | collective-permute-start | bytes 196616 | tf_op jit(solution)/shard_map/ppermute | solution.py:19
  49.5 20.4 %all-to-all-start.1 = ((bf16[64,4,128]{2,1,0:T(4,128)(2,1)}), bf16[64,4,128]{2,1,0:T(4,128)(2,1)S(1)}, u32[]{:S(2)}, u32[]{:S(2)}) async-start(bf16[64,4,128]{2,1,0:T(4,128)(2,1)} %bitcast.10), calls=%async_computation.1 | async-start | bytes 131072 | tf_op jit(solution)/shard_map/all_to_all | solution.py:102
